TPU v7x, 128 devices: a whole 4x4x4 slice. The times are simulated.
128 devices in a mesh: clu: 8 (over y, x_hi), mem: 16 (over x_lo, z, core).
Axes of the slice: x: 4 (x_hi: 2, x_lo: 2; x = x_hi * 2 + x_lo), y: 4, z: 4, core: 2. Of those that a mesh axis runs over, the one named last changes fastest.
Arguments:
- embeddings: bfloat16 [131072, 768], P(('clu', 'mem'))
- block_order: int32 [8, 128], P('clu'), may hold values from 0 to 7, as said below
Outputs:
- weight: float32 [131072], P(('clu', 'mem'))
Inputs may be any that keep to these rules, and one draw needn't show every extreme that they name: `block_order`: each aligned run of 8 entries is a permutation of 0 to 7.
All inputs are finite; a program needn't handle non-finite values.
Results may differ from a plain program's by a relative error of at most 0.0029.
Values may be sent and summed in bfloat16 or wider, within the bound.
No kernel may reach another device: no remote copies, remote signals or barrier semaphores. Data moves between devices by JAX's collectives and lax.ppermute only.
A program may use at most 64 MiB of HBM per device.

v0:
```python
import itertools

import jax
import jax.numpy as jnp
from jax import lax
from jax.sharding import PartitionSpec as P


BLK = 128


def squared(values):
    return jnp.sum(jnp.square(values.astype(jnp.float32)), axis=1)


def class_spans(count):
    spans = []
    start = 0
    width = count // 2
    while start < count:
        end = min(start + max(width, 1), count)
        spans.append((start, end))
        start = end
        width //= 2
    return spans


def member_ring(count):
    if count != 16:
        return list(range(count))
    chips = [(0, 0), (0, 1), (0, 2), (0, 3), (1, 3), (1, 2), (1, 1), (1, 0)]
    return [x * 8 + z * 2 + core for core in (0, 1) for x, z in chips]


def cover(count):
    if count == 16:
        return (0, 1, 5, 8, 15)
    best = None
    half = count // 2
    for size in range(2, count + 1):
        for rest in itertools.combinations(range(1, count), size - 1):
            offsets = (0,) + rest
            kinds = set()
            for a, b in itertools.combinations(offsets, 2):
                step = (b - a) % count
                kinds.add(min(step, count - step))
            if kinds >= set(range(1, half + 1)):
                cost = sum(min(d, count - d) for d in rest)
                if best is None or cost < best[0]:
                    best = (cost, offsets)
        if best is not None:
            return best[1]
    return tuple(range(count))


def plan(count):
    offsets = cover(count)
    pairs = []
    for step in range(1, count // 2 + 1):
        for a, b in itertools.permutations(offsets, 2):
            if (b - a) % count == step:
                pairs.append((a, b, 2 * step != count))
                break
    return offsets, pairs


def grand_total(value, axes, size):
    spread = lax.all_to_all(jnp.broadcast_to(value, (size, 1)), axes, 0, 0, tiled=True)
    return jnp.sum(spread)


def kernel_sums(left, right, left_norms, right_norms, both):
    products = lax.dot_general(
        left, right, (((1,), (1,)), ((), ())), preferred_element_type=jnp.float32
    )
    distance = left_norms[:, None] + right_norms[None, :] - 2.0 * products
    kernel = jnp.exp(-0.5 * distance)
    rows = jnp.sum(kernel, axis=1)
    cols = jnp.sum(kernel, axis=0) if both else None
    return rows, cols


def shards(embeddings, block_order):
    row_count, width = embeddings.shape
    member_count = lax.axis_size("mem")
    position = lax.axis_index("mem")
    per_device = row_count // BLK
    order = lax.dynamic_slice_in_dim(block_order[0], position * per_device, per_device)
    blocks = embeddings.reshape(per_device, BLK, width)
    ordered = jnp.take(blocks, order, axis=0).reshape(row_count, width)
    spans = [(start * BLK, end * BLK) for start, end in class_spans(per_device)]

    ring = member_ring(member_count)
    offsets, pairs = plan(member_count)

    def fetch(value, offset):
        return lax.ppermute(
            value,
            "mem",
            [(ring[(r + offset) % member_count], ring[r]) for r in range(member_count)],
        )

    def give_back(value, offset):
        return lax.ppermute(
            value,
            "mem",
            [(ring[r], ring[(r + offset) % member_count]) for r in range(member_count)],
        )

    late = offsets[-1]
    held = {0: ordered}
    for offset in [late] + [o for o in offsets[1:] if o != late]:
        held[offset] = fetch(ordered, offset)
    norms = {}
    partial = {offset: [None] * len(spans) for offset in offsets}

    def add(offset, index, value):
        slot = partial[offset]
        slot[index] = value if slot[index] is None else slot[index] + value

    def blocks(chosen):
        for offset in {o for a, b, _ in chosen for o in (a, b)} | {0}:
            if offset not in norms:
                norms[offset] = squared(held[offset])
        for index, (start, end) in enumerate(spans):
            for a, b, both in chosen:
                rows, cols = kernel_sums(
                    held[a][start:end], held[b][start:end],
                    norms[a][start:end], norms[b][start:end], both,
                )
                add(a, index, rows)
                if both:
                    add(b, index, cols)

    blocks([(0, 0, False)] + [p for p in pairs if late not in p[:2]])
    blocks([p for p in pairs if late in p[:2]])

    gathered = {}
    for offset in offsets:
        parts = [
            value if value is not None else jnp.zeros((end - start,), jnp.float32)
            for value, (start, end) in zip(partial[offset], spans)
        ]
        gathered[offset] = jnp.concatenate(parts)
    density = gathered[0]
    for offset in offsets[1:]:
        density = density + give_back(gathered[offset], offset)

    inverse = 1.0 / density.reshape(per_device, BLK)
    total = grand_total(jnp.sum(inverse), ("clu", "mem"), lax.axis_size("clu") * member_count)
    everything = jnp.float32(row_count * lax.axis_size("clu") * member_count)
    weight = inverse * (everything / total)
    spots = jnp.arange(per_device, dtype=jnp.int32)
    back = jnp.sum(
        jnp.where(order[None, :] == spots[:, None], spots[None, :], 0), axis=1
    )
    return jnp.take(weight, back, axis=0).reshape(-1)


def solution(mesh):
    placed = (P(("clu", "mem"), None), P("clu", None))
    return jax.shard_map(
        shards, mesh=mesh, in_specs=placed, out_specs=P(("clu", "mem")), check_vma=False
    )
```

profile of v0, /device:TPU:0, one launch (start us, length us, event | category | flops | bytes accessed | tf_op | source)
XLA Modules:
  0.0 120.5 jit_solution(2924311025257094175)
XLA Ops:
  0.0 0.8 fusion.144
  0.9 0.7 compare_and_fusion
  1.7 0.6 gather_fusion
  2.6 1.1 collective-permute-start
  3.8 2.7 %collective-permute-start.1 = (bf16[1024,768]{1,0:T(8,128)(2,1)S(1)}, bf16[1024,768]{1,0:T(8,128)(2,1)S(1)}, u32[]{:S(2)}, u32[]{:S(2)}) collective-permute-start(bf16[1024,768]{1,0:T(8,128)(2,1)S(1)} %bitcast_select_fusion), channel_id=1, source_target_pairs={{12,0},{10,2},{8,4},{1,6},{3,14},{5,12},{7,10},{15,8},{13,1},{11,3... | collective-permute-start | bytes 4718600 | tf_op jit(solution)/shard_map/ppermute | solution.py:97
  6.4 1.9 %collective-permute-start.3 = (bf16[1024,768]{1,0:T(8,128)(2,1)S(1)}, bf16[1024,768]{1,0:T(8,128)(2,1)S(1)}, u32[]{:S(2)}, u32[]{:S(2)}) collective-permute-start(bf16[1024,768]{1,0:T(8,128)(2,1)S(1)} %bitcast_select_fusion), channel_id=1, source_target_pairs={{9,0},{0,2},{2,4},{4,6},{6,14},{14,12},{12,10},{10,8},{8,1},{1,3},... | collective-permute-start | bytes 4718600 | tf_op jit(solution)/shard_map/ppermute | solution.py:97
  8.3 0.7 collective-permute-start.2
  9.0 0.6 multiply_reduce_fusion.4
  10.7 0.7 fusion.3
  11.4 27.7 %collective-permute-done = bf16[1024,768]{1,0:T(8,128)(2,1)S(1)} collective-permute-done((bf16[1024,768]{1,0:T(8,128)(2,1)S(1)}, bf16[1024,768]{1,0:T(8,128)(2,1)S(1)}, u32[]{:S(2)}, u32[]{:S(2)}) %collective-permute-start) | collective-permute-done | bytes 1572896 | tf_op jit(solution)/shard_map/ppermute | solution.py:97
  39.5 3.9 %collective-permute-done.1 = bf16[1024,768]{1,0:T(8,128)(2,1)S(1)} collective-permute-done((bf16[1024,768]{1,0:T(8,128)(2,1)S(1)}, bf16[1024,768]{1,0:T(8,128)(2,1)S(1)}, u32[]{:S(2)}, u32[]{:S(2)}) %collective-permute-start.1) | collective-permute-done | bytes 1572896 | tf_op jit(solution)/shard_map/ppermute | solution.py:97
  43.9 31.2 %collective-permute-done.3 = bf16[1024,768]{1,0:T(8,128)(2,1)S(1)} collective-permute-done((bf16[1024,768]{1,0:T(8,128)(2,1)S(1)}, bf16[1024,768]{1,0:T(8,128)(2,1)S(1)}, u32[]{:S(2)}, u32[]{:S(2)}) %collective-permute-start.3) | collective-permute-done | bytes 1572896 | tf_op jit(solution)/shard_map/ppermute | solution.py:97
  80.2 0.6 convolution_multiply_fusion.6
  80.8 0.6 convolution_multiply_fusion.4
  81.5 0.6 convolution_multiply_fusion
  82.1 0.6 convolution_multiply_fusion.2
  82.7 0.6 convolution_multiply_fusion.1
  83.3 0.6 convolution_multiply_fusion.3
  84.0 2.3 %fusion.17 = (f32[512]{0:T(512)S(1)}, f32[512]{0:T(512)S(1)}, f32[512]{0:T(512)S(1)}, f32[512]{0:T(512)S(1)}, f32[512]{0:T(512)S(1)}, /*index=5*/f32[512]{0:T(51...) fusion(f32[512]{0:T(512)S(1)} %slice-done, ...), kind=kOutput, calls=%fused_computation.70 | convolution fusion | flops 412083200 | bytes 7907328 | tf_op jit(solution)/shard_map/dot_general | solution.py:73
  86.3 1.7 %collective-permute-start.7 = (f32[1024]{0:T(1024)S(1)}, f32[1024]{0:T(1024)S(1)}, u32[]{:S(2)}, u32[]{:S(2)}) collective-permute-start(f32[1024]{0:T(1024)S(1)} %pad_maximum_fusion.3), channel_id=1, source_target_pairs={{0,9},{2,0},{4,2},{6,4},{14,6},{12,14},{10,12},{8,10},{1,8},{3,1},... | collective-permute-start | bytes 12296 | tf_op jit(solution)/shard_map/ppermute | solution.py:104
  88.9 1.5 %collective-permute-start.6 = (f32[1024]{0:T(1024)S(1)}, f32[1024]{0:T(1024)S(1)}, u32[]{:S(2)}, u32[]{:S(2)}) collective-permute-start(f32[1024]{0:T(1024)S(1)} %pad_maximum_fusion.2), channel_id=1, source_target_pairs={{0,1},{2,3},{4,5},{6,7},{14,15},{12,13},{10,11},{8,9},{1,0},{3,2},... | collective-permute-start | bytes 12296 | tf_op jit(solution)/shard_map/ppermute | solution.py:104
  90.8 0.4 fusion.149
  91.3 3.2 %collective-permute-start.5 = (f32[1024]{0:T(1024)S(1)}, f32[1024]{0:T(1024)S(1)}, u32[]{:S(2)}, u32[]{:S(2)}) collective-permute-start(f32[1024]{0:T(1024)S(1)} %pad_maximum_fusion.1), channel_id=1, source_target_pairs={{0,12},{2,10},{4,8},{6,1},{14,3},{12,5},{10,7},{8,15},{1,13},{3,11... | collective-permute-start | bytes 12296 | tf_op jit(solution)/shard_map/ppermute | solution.py:104
  95.5 0.7 exponential_reduce_fusion
  96.7 1.4 %collective-permute-done.4 = f32[1024]{0:T(1024)S(1)} collective-permute-done((f32[1024]{0:T(1024)S(1)}, f32[1024]{0:T(1024)S(1)}, u32[]{:S(2)}, u32[]{:S(2)}) %collective-permute-start.4) | collective-permute-done | bytes 4128 | tf_op jit(solution)/shard_map/ppermute | solution.py:104
  98.1 0.6 fusion.154
  98.7 1.3 %broadcast_in_dim.44 = f32[128,1,1]{2,1,0:T(1,128)} broadcast(f32[]{:T(128)} %get-tuple-element.97), dimensions={} | broadcast | bytes 516 | tf_op jit(solution)/shard_map/broadcast_in_dim | solution.py:68
  100.0 8.2 %all-to-all-start = ((f32[128,1,1]{2,1,0:T(1,128)}), f32[128,1,1]{2,1,0:T(1,128)S(1)}, u32[]{:S(2)}, u32[]{:S(2)}) async-start(f32[128,1,1]{2,1,0:T(1,128)} %broadcast_in_dim.44), calls=%async_computation | async-start | bytes 131072 | tf_op jit(solution)/shard_map/all_to_all | solution.py:68
  108.3 9.5 %all-to-all-done = f32[128,1,1]{2,1,0:T(1,128)S(1)} async-done(((f32[128,1,1]{2,1,0:T(1,128)}), f32[128,1,1]{2,1,0:T(1,128)S(1)}, u32[]{:S(2)}, u32[]{:S(2)}) %all-to-all-start) | async-done | bytes 544 | tf_op jit(solution)/shard_map/all_to_all | solution.py:68
  117.8 0.7 reduce_sum.721
  119.3 0.6 gather_fusion.1
  119.8 0.7 select_bitcast_fusion
  (92 shorter events, 10.0 us)
Async XLA Ops:
  0.0 1.7 %copy-start = (bf16[1024,768]{1,0:T(8,128)(2,1)S(1)}, bf16[1024,768]{1,0:T(8,128)(2,1)}, u32[]{:S(2)}) copy-start(bf16[1024,768]{1,0:T(8,128)(2,1)} %param.2) | copy-start | bytes 4718596
  2.6 36.5 %collective-permute-start = (bf16[1024,768]{1,0:T(8,128)(2,1)S(1)}, bf16[1024,768]{1,0:T(8,128)(2,1)S(1)}, u32[]{:S(2)}, u32[]{:S(2)}) collective-permute-start(bf16[1024,768]{1,0:T(8,128)(2,1)S(1)} %bitcast_select_fusion), channel_id=1, source_target_pairs={{2,0},{4,2},{6,4},{14,6},{12,14},{10,12},{8,10},{1,8},{3,1},{5,3},... | collective-permute-start | bytes 4718600 | tf_op jit(solution)/shard_map/ppermute | solution.py:97
  3.8 39.7 %collective-permute-start.1 = (bf16[1024,768]{1,0:T(8,128)(2,1)S(1)}, bf16[1024,768]{1,0:T(8,128)(2,1)S(1)}, u32[]{:S(2)}, u32[]{:S(2)}) collective-permute-start(bf16[1024,768]{1,0:T(8,128)(2,1)S(1)} %bitcast_select_fusion), channel_id=1, source_target_pairs={{12,0},{10,2},{8,4},{1,6},{3,14},{5,12},{7,10},{15,8},{13,1},{11,3... | collective-permute-start | bytes 4718600 | tf_op jit(solution)/shard_map/ppermute | solution.py:97
  6.4 68.6 %collective-permute-start.3 = (bf16[1024,768]{1,0:T(8,128)(2,1)S(1)}, bf16[1024,768]{1,0:T(8,128)(2,1)S(1)}, u32[]{:S(2)}, u32[]{:S(2)}) collective-permute-start(bf16[1024,768]{1,0:T(8,128)(2,1)S(1)} %bitcast_select_fusion), channel_id=1, source_target_pairs={{9,0},{0,2},{2,4},{4,6},{6,14},{14,12},{12,10},{10,8},{8,1},{1,3},... | collective-permute-start | bytes 4718600 | tf_op jit(solution)/shard_map/ppermute | solution.py:97
  8.3 67.2 %collective-permute-start.2 = (bf16[1024,768]{1,0:T(8,128)(2,1)S(1)}, bf16[1024,768]{1,0:T(8,128)(2,1)S(1)}, u32[]{:S(2)}, u32[]{:S(2)}) collective-permute-start(bf16[1024,768]{1,0:T(8,128)(2,1)S(1)} %bitcast_select_fusion), channel_id=1, source_target_pairs={{1,0},{3,2},{5,4},{7,6},{15,14},{13,12},{11,10},{9,8},{0,1},{2,3},... | collective-permute-start | bytes 4718600 | tf_op jit(solution)/shard_map/ppermute | solution.py:97
  39.5 35.9 %copy-start.1 = (f32[1024]{0:T(1024)}, f32[1024]{0:T(1024)S(1)}, u32[]{:S(2)}) copy-start(f32[1024]{0:T(1024)S(1)} %multiply_reduce_fusion.3) | copy-start | bytes 12292
  43.8 32.0 %copy-start.2 = (f32[1024]{0:T(1024)}, f32[1024]{0:T(1024)S(1)}, u32[]{:S(2)}) copy-start(f32[1024]{0:T(1024)S(1)} %multiply_reduce_fusion.2) | copy-start | bytes 12292
  75.4 1.4 %copy-start.3 = (f32[1024]{0:T(1024)}, f32[1024]{0:T(1024)S(1)}, u32[]{:S(2)}) copy-start(f32[1024]{0:T(1024)S(1)} %multiply_reduce_fusion) | copy-start | bytes 12292
  83.3 0.7 slice-start
  83.3 0.7 slice-start.1
  83.3 0.7 slice-start.2
  86.3 10.4 %collective-permute-start.7 = (f32[1024]{0:T(1024)S(1)}, f32[1024]{0:T(1024)S(1)}, u32[]{:S(2)}, u32[]{:S(2)}) collective-permute-start(f32[1024]{0:T(1024)S(1)} %pad_maximum_fusion.3), channel_id=1, source_target_pairs={{0,9},{2,0},{4,2},{6,4},{14,6},{12,14},{10,12},{8,10},{1,8},{3,1},... | collective-permute-start | bytes 12296 | tf_op jit(solution)/shard_map/ppermute | solution.py:104
  88.9 7.8 %collective-permute-start.6 = (f32[1024]{0:T(1024)S(1)}, f32[1024]{0:T(1024)S(1)}, u32[]{:S(2)}, u32[]{:S(2)}) collective-permute-start(f32[1024]{0:T(1024)S(1)} %pad_maximum_fusion.2), channel_id=1, source_target_pairs={{0,1},{2,3},{4,5},{6,7},{14,15},{12,13},{10,11},{8,9},{1,0},{3,2},... | collective-permute-start | bytes 12296 | tf_op jit(solution)/shard_map/ppermute | solution.py:104
  91.3 5.4 %collective-permute-start.5 = (f32[1024]{0:T(1024)S(1)}, f32[1024]{0:T(1024)S(1)}, u32[]{:S(2)}, u32[]{:S(2)}) collective-permute-start(f32[1024]{0:T(1024)S(1)} %pad_maximum_fusion.1), channel_id=1, source_target_pairs={{0,12},{2,10},{4,8},{6,1},{14,3},{12,5},{10,7},{8,15},{1,13},{3,11... | collective-permute-start | bytes 12296 | tf_op jit(solution)/shard_map/ppermute | solution.py:104
  95.0 3.1 %collective-permute-start.4 = (f32[1024]{0:T(1024)S(1)}, f32[1024]{0:T(1024)S(1)}, u32[]{:S(2)}, u32[]{:S(2)}) collective-permute-start(f32[1024]{0:T(1024)S(1)} %pad_maximum_fusion), channel_id=1, source_target_pairs={{0,2},{2,4},{4,6},{6,14},{14,12},{12,10},{10,8},{8,1},{1,3},{3,5},... | collective-permute-start | bytes 12296 | tf_op jit(solution)/shard_map/ppermute | solution.py:104
  100.0 17.8 %all-to-all-start = ((f32[128,1,1]{2,1,0:T(1,128)}), f32[128,1,1]{2,1,0:T(1,128)S(1)}, u32[]{:S(2)}, u32[]{:S(2)}) async-start(f32[128,1,1]{2,1,0:T(1,128)} %broadcast_in_dim.44), calls=%async_computation | async-start | bytes 131072 | tf_op jit(solution)/shard_map/all_to_all | solution.py:68
where the time goes:
time: 121 us; the launch traced here: 120 us
  waiting for transfers between devices  73.7 us (61%)
  starting transfers between devices  21.1 us (17%)
  matrix products  15.3 us (13%)
  other arithmetic  6.29 us (5%)
  local copies, waits for them, and re-layouts  2.79 us (2%)
  between operations  1.29 us (1%)
    ppermute x4, waiting for transfers between devices, fetch(): lax.ppermute(value, 'mem', [(ring[(r + offset) % member_count], ring[r])...  62.8 us
    dot_general x36, matrix products, kernel_sums(): lax.dot_general(left, right, (((1,), (1,)), ((), ())), preferred_element_...  15.3 us
    all_to_all x1, waiting for transfers between devices, grand_total(): lax.all_to_all(jnp.broadcast_to(value, (size, 1)), axes, 0, 0, tiled=True)  9.53 us
    all_to_all x1, starting transfers between devices, grand_total(): lax.all_to_all(jnp.broadcast_to(value, (size, 1)), axes, 0, 0, tiled=True)  8.25 us
    ppermute x4, starting transfers between devices, give_back(): lax.ppermute(value, 'mem', [(ring[r], ring[(r + offset) % member_count])...  6.51 us
    ppermute x4, starting transfers between devices, fetch(): lax.ppermute(value, 'mem', [(ring[(r + offset) % member_count], ring[r])...  6.37 us
  transfers between devices with their start and end apart: 9, of which 5 were waited for; matrix products, arithmetic and copies ran while one was open for 6% of the time, Pallas kernels for 0%

commit v1 on v0

--- a/solution.py
+++ b/solution.py
@@ -109,7 +109,7 @@
 
     late = offsets[-1]
     held = {0: ordered}
-    for offset in [late] + [o for o in offsets[1:] if o != late]:
+    for offset in offsets[1:]:
         held[offset] = fetch(ordered, offset)
     norms = {}
     partial = {offset: [None] * len(spans) for offset in offsets}
@@ -132,19 +132,21 @@
                 if both:
                     add(b, index, cols)
 
+    late_pairs = [p for p in pairs if late in p[:2]]
     blocks([(0, 0, False)] + [p for p in pairs if late not in p[:2]])
-    blocks([p for p in pairs if late in p[:2]])
+    partial = lax.optimization_barrier(partial)
+    blocks(late_pairs)
 
-    gathered = {}
-    for offset in offsets:
+    def joined(offset):
         parts = [
             value if value is not None else jnp.zeros((end - start,), jnp.float32)
             for value, (start, end) in zip(partial[offset], spans)
         ]
-        gathered[offset] = jnp.concatenate(parts)
-    density = gathered[0]
+        return jnp.concatenate(parts)
+
+    density = joined(0)
     for offset in offsets[1:]:
-        density = density + give_back(gathered[offset], offset)
+        density = density + give_back(joined(offset), offset)
 
     inverse = 1.0 / density.reshape(per_device, BLK)
     total = grand_total(jnp.sum(inverse), ("clu", "mem"), lax.axis_size("clu") * member_count)

time: 121 us -> 122 us (level)
  starting transfers between devices: 21.1 us -> 51.2 us
  waiting for transfers between devices: 73.7 us -> 44.6 us
    ppermute x4, waiting for transfers between devices: 62.8 us -> 31.5 us  [fetch(): lax.ppermute(value, 'mem', [(ring[(r + offset) % member_count], ring[r])...]
    ppermute x4, starting transfers between devices: 6.51 us -> 36.1 us  [give_back(): lax.ppermute(value, 'mem', [(ring[r], ring[(r + offset) % member_count])...]
    ppermute x4, waiting for transfers between devices: 1.39 us -> 3.57 us  [give_back(): lax.ppermute(value, 'mem', [(ring[r], ring[(r + offset) % member_count])...]
  transfers between devices with their start and end apart: 9 -> 9, of which waited for: 5 -> 6; matrix products, arithmetic and copies ran while one was open for 6% -> 4% of each run, Pallas kernels for 0% -> 0%
where the time goes in v1:
time: 122 us; the launch traced here: 121 us
  starting transfers between devices  51.2 us (42%)
  waiting for transfers between devices  44.6 us (37%)
  matrix products  15.1 us (12%)
  other arithmetic  6.31 us (5%)
  local copies, waits for them, and re-layouts  2.8 us (2%)
  between operations  1.32 us (1%)
    ppermute x4, starting transfers between devices, give_back(): lax.ppermute(value, 'mem', [(ring[r], ring[(r + offset) % member_count])...  36.1 us
    ppermute x4, waiting for transfers between devices, fetch(): lax.ppermute(value, 'mem', [(ring[(r + offset) % member_count], ring[r])...  31.5 us
    dot_general x36, matrix products, kernel_sums(): lax.dot_general(left, right, (((1,), (1,)), ((), ())), preferred_element_...  15.1 us
    all_to_all x1, waiting for transfers between devices, grand_total(): lax.all_to_all(jnp.broadcast_to(value, (size, 1)), axes, 0, 0, tiled=True)  9.53 us
    all_to_all x1, starting transfers between devices, grand_total(): lax.all_to_all(jnp.broadcast_to(value, (size, 1)), axes, 0, 0, tiled=True)  8.1 us
    ppermute x4, starting transfers between devices, fetch(): lax.ppermute(value, 'mem', [(ring[(r + offset) % member_count], ring[r])...  6.98 us
    ppermute x4, waiting for transfers between devices, give_back(): lax.ppermute(value, 'mem', [(ring[r], ring[(r + offset) % member_count])...  3.57 us
  transfers between devices with their start and end apart: 9, of which 6 were waited for; matrix products, arithmetic and copies ran while one was open for 4% of the time, Pallas kernels for 0%

profile of v1, /device:TPU:0, one launch (start us, length us, event | category | flops | bytes accessed | tf_op | source)
XLA Modules:
  0.0 121.2 jit_solution(5453033213952132864)
XLA Ops:
  0.0 0.8 fusion.144
  0.9 0.7 compare_and_fusion
  1.7 0.6 gather_fusion
  2.6 2.1 %collective-permute-start.3 = (bf16[1024,768]{1,0:T(8,128)(2,1)S(1)}, bf16[1024,768]{1,0:T(8,128)(2,1)S(1)}, u32[]{:S(2)}, u32[]{:S(2)}) collective-permute-start(bf16[1024,768]{1,0:T(8,128)(2,1)S(1)} %bitcast_select_fusion), channel_id=1, source_target_pairs={{9,0},{0,2},{2,4},{4,6},{6,14},{14,12},{12,10},{10,8},{8,1},{1,3},... | collective-permute-start | bytes 4718600 | tf_op jit(solution)/shard_map/ppermute | solution.py:97
  4.7 3.7 %collective-permute-start.1 = (bf16[1024,768]{1,0:T(8,128)(2,1)S(1)}, bf16[1024,768]{1,0:T(8,128)(2,1)S(1)}, u32[]{:S(2)}, u32[]{:S(2)}) collective-permute-start(bf16[1024,768]{1,0:T(8,128)(2,1)S(1)} %bitcast_select_fusion), channel_id=1, source_target_pairs={{12,0},{10,2},{8,4},{1,6},{3,14},{5,12},{7,10},{15,8},{13,1},{11,3... | collective-permute-start | bytes 4718600 | tf_op jit(solution)/shard_map/ppermute | solution.py:97
  8.5 1.2 collective-permute-start
  9.6 0.6 multiply_reduce_fusion.4
  11.3 0.7 fusion.3
  12.0 27.2 %collective-permute-done.3 = bf16[1024,768]{1,0:T(8,128)(2,1)S(1)} collective-permute-done((bf16[1024,768]{1,0:T(8,128)(2,1)S(1)}, bf16[1024,768]{1,0:T(8,128)(2,1)S(1)}, u32[]{:S(2)}, u32[]{:S(2)}) %collective-permute-start.3) | collective-permute-done | bytes 1572896 | tf_op jit(solution)/shard_map/ppermute | solution.py:97
  40.1 4.0 %collective-permute-done.1 = bf16[1024,768]{1,0:T(8,128)(2,1)S(1)} collective-permute-done((bf16[1024,768]{1,0:T(8,128)(2,1)S(1)}, bf16[1024,768]{1,0:T(8,128)(2,1)S(1)}, u32[]{:S(2)}, u32[]{:S(2)}) %collective-permute-start.1) | collective-permute-done | bytes 1572896 | tf_op jit(solution)/shard_map/ppermute | solution.py:97
  45.2 0.4 fusion.150
  49.5 0.6 convolution_multiply_fusion.2
  50.1 0.6 convolution_multiply_fusion
  50.7 0.6 convolution_multiply_fusion.6
  51.3 0.6 convolution_multiply_fusion.4
  51.9 0.6 convolution_multiply_fusion.3
  52.6 0.6 convolution_multiply_fusion.7
  53.2 2.1 %fusion.27 = (f32[512]{0:T(512)S(1)}, f32[512]{0:T(512)S(1)}, f32[512]{0:T(512)S(1)}, f32[512]{0:T(512)S(1)}, f32[512]{0:T(512)S(1)}, /*index=5*/f32[512]{0:T(51...) fusion(f32[512]{0:T(512)S(1)} %slice-done, ...), kind=kOutput, calls=%fused_computation.80 | convolution fusion | flops 412083200 | bytes 7907328 | tf_op jit(solution)/shard_map/dot_general | solution.py:73
  55.3 0.4 fusion.153
  56.2 0.7 exponential_reduce_fusion
  57.3 0.4 fusion.152
  59.1 30.6 %collective-permute-start.4 = (f32[1024]{0:T(1024)S(1)}, f32[1024]{0:T(1024)S(1)}, u32[]{:S(2)}, u32[]{:S(2)}) collective-permute-start(f32[1024]{0:T(1024)S(1)} %pad_maximum_fusion), channel_id=1, source_target_pairs={{0,2},{2,4},{4,6},{6,14},{14,12},{12,10},{10,8},{8,1},{1,3},{3,5},... | collective-permute-start | bytes 12296 | tf_op jit(solution)/shard_map/ppermute | solution.py:104
  90.2 5.1 %collective-permute-start.5 = (f32[1024]{0:T(1024)S(1)}, f32[1024]{0:T(1024)S(1)}, u32[]{:S(2)}, u32[]{:S(2)}) collective-permute-start(f32[1024]{0:T(1024)S(1)} %pad_maximum_fusion.1), channel_id=1, source_target_pairs={{0,12},{2,10},{4,8},{6,1},{14,3},{12,5},{10,7},{8,15},{1,13},{3,11... | collective-permute-start | bytes 12296 | tf_op jit(solution)/shard_map/ppermute | solution.py:104
  95.4 1.2 collective-permute-done.5
  96.6 2.4 %collective-permute-done.7 = f32[1024]{0:T(1024)S(1)} collective-permute-done((f32[1024]{0:T(1024)S(1)}, f32[1024]{0:T(1024)S(1)}, u32[]{:S(2)}, u32[]{:S(2)}) %collective-permute-start.7) | collective-permute-done | bytes 4128 | tf_op jit(solution)/shard_map/ppermute | solution.py:104
  99.0 0.6 fusion.154
  99.6 1.3 %broadcast_in_dim.44 = f32[128,1,1]{2,1,0:T(1,128)} broadcast(f32[]{:T(128)} %get-tuple-element.129), dimensions={} | broadcast | bytes 516 | tf_op jit(solution)/shard_map/broadcast_in_dim | solution.py:68
  100.9 8.1 %all-to-all-start = ((f32[128,1,1]{2,1,0:T(1,128)}), f32[128,1,1]{2,1,0:T(1,128)S(1)}, u32[]{:S(2)}, u32[]{:S(2)}) async-start(f32[128,1,1]{2,1,0:T(1,128)} %broadcast_in_dim.44), calls=%async_computation | async-start | bytes 131072 | tf_op jit(solution)/shard_map/all_to_all | solution.py:68
  109.0 9.5 %all-to-all-done = f32[128,1,1]{2,1,0:T(1,128)S(1)} async-done(((f32[128,1,1]{2,1,0:T(1,128)}), f32[128,1,1]{2,1,0:T(1,128)S(1)}, u32[]{:S(2)}, u32[]{:S(2)}) %all-to-all-start) | async-done | bytes 544 | tf_op jit(solution)/shard_map/all_to_all | solution.py:68
  118.5 0.7 reduce_sum.721
  120.0 0.6 gather_fusion.1
  120.5 0.7 select_bitcast_fusion
  (98 shorter events, 9.7 us)
Async XLA Ops:
  0.0 1.7 %copy-start = (bf16[1024,768]{1,0:T(8,128)(2,1)S(1)}, bf16[1024,768]{1,0:T(8,128)(2,1)}, u32[]{:S(2)}) copy-start(bf16[1024,768]{1,0:T(8,128)(2,1)} %param.2) | copy-start | bytes 4718596
  2.6 36.6 %collective-permute-start.3 = (bf16[1024,768]{1,0:T(8,128)(2,1)S(1)}, bf16[1024,768]{1,0:T(8,128)(2,1)S(1)}, u32[]{:S(2)}, u32[]{:S(2)}) collective-permute-start(bf16[1024,768]{1,0:T(8,128)(2,1)S(1)} %bitcast_select_fusion), channel_id=1, source_target_pairs={{9,0},{0,2},{2,4},{4,6},{6,14},{14,12},{12,10},{10,8},{8,1},{1,3},... | collective-permute-start | bytes 4718600 | tf_op jit(solution)/shard_map/ppermute | solution.py:97
  4.7 34.9 %collective-permute-start.2 = (bf16[1024,768]{1,0:T(8,128)(2,1)S(1)}, bf16[1024,768]{1,0:T(8,128)(2,1)S(1)}, u32[]{:S(2)}, u32[]{:S(2)}) collective-permute-start(bf16[1024,768]{1,0:T(8,128)(2,1)S(1)} %bitcast_select_fusion), channel_id=1, source_target_pairs={{1,0},{3,2},{5,4},{7,6},{15,14},{13,12},{11,10},{9,8},{0,1},{2,3},... | collective-permute-start | bytes 4718600 | tf_op jit(solution)/shard_map/ppermute | solution.py:97
  4.7 39.3 %collective-permute-start.1 = (bf16[1024,768]{1,0:T(8,128)(2,1)S(1)}, bf16[1024,768]{1,0:T(8,128)(2,1)S(1)}, u32[]{:S(2)}, u32[]{:S(2)}) collective-permute-start(bf16[1024,768]{1,0:T(8,128)(2,1)S(1)} %bitcast_select_fusion), channel_id=1, source_target_pairs={{12,0},{10,2},{8,4},{1,6},{3,14},{5,12},{7,10},{15,8},{13,1},{11,3... | collective-permute-start | bytes 4718600 | tf_op jit(solution)/shard_map/ppermute | solution.py:97
  8.5 36.3 %collective-permute-start = (bf16[1024,768]{1,0:T(8,128)(2,1)S(1)}, bf16[1024,768]{1,0:T(8,128)(2,1)S(1)}, u32[]{:S(2)}, u32[]{:S(2)}) collective-permute-start(bf16[1024,768]{1,0:T(8,128)(2,1)S(1)} %bitcast_select_fusion), channel_id=1, source_target_pairs={{2,0},{4,2},{6,4},{14,6},{12,14},{10,12},{8,10},{1,8},{3,1},{5,3},... | collective-permute-start | bytes 4718600 | tf_op jit(solution)/shard_map/ppermute | solution.py:97
  39.6 4.8 %copy-start.1 = (f32[1024]{0:T(1024)}, f32[1024]{0:T(1024)S(1)}, u32[]{:S(2)}) copy-start(f32[1024]{0:T(1024)S(1)} %multiply_reduce_fusion) | copy-start | bytes 12292
  44.4 1.2 copy-start.2
  45.1 0.9 copy-start.3
  52.5 0.7 slice-start
  52.5 0.7 slice-start.1
  52.5 0.7 slice-start.2
  58.3 37.1 %collective-permute-start.6 = (f32[1024]{0:T(1024)S(1)}, f32[1024]{0:T(1024)S(1)}, u32[]{:S(2)}, u32[]{:S(2)}) collective-permute-start(f32[1024]{0:T(1024)S(1)} %pad_maximum_fusion.2), channel_id=1, source_target_pairs={{0,1},{2,3},{4,5},{6,7},{14,15},{12,13},{10,11},{8,9},{1,0},{3,2},... | collective-permute-start | bytes 12296 | tf_op jit(solution)/shard_map/ppermute | solution.py:104
  59.1 36.3 %collective-permute-start.4 = (f32[1024]{0:T(1024)S(1)}, f32[1024]{0:T(1024)S(1)}, u32[]{:S(2)}, u32[]{:S(2)}) collective-permute-start(f32[1024]{0:T(1024)S(1)} %pad_maximum_fusion), channel_id=1, source_target_pairs={{0,2},{2,4},{4,6},{6,14},{14,12},{12,10},{10,8},{8,1},{1,3},{3,5},... | collective-permute-start | bytes 12296 | tf_op jit(solution)/shard_map/ppermute | solution.py:104
  90.2 6.4 %collective-permute-start.5 = (f32[1024]{0:T(1024)S(1)}, f32[1024]{0:T(1024)S(1)}, u32[]{:S(2)}, u32[]{:S(2)}) collective-permute-start(f32[1024]{0:T(1024)S(1)} %pad_maximum_fusion.1), channel_id=1, source_target_pairs={{0,12},{2,10},{4,8},{6,1},{14,3},{12,5},{10,7},{8,15},{1,13},{3,11... | collective-permute-start | bytes 12296 | tf_op jit(solution)/shard_map/ppermute | solution.py:104
  95.3 3.7 %collective-permute-start.7 = (f32[1024]{0:T(1024)S(1)}, f32[1024]{0:T(1024)S(1)}, u32[]{:S(2)}, u32[]{:S(2)}) collective-permute-start(f32[1024]{0:T(1024)S(1)} %pad_maximum_fusion.3), channel_id=1, source_target_pairs={{0,9},{2,0},{4,2},{6,4},{14,6},{12,14},{10,12},{8,10},{1,8},{3,1},... | collective-permute-start | bytes 12296 | tf_op jit(solution)/shard_map/ppermute | solution.py:104
  100.9 17.7 %all-to-all-start = ((f32[128,1,1]{2,1,0:T(1,128)}), f32[128,1,1]{2,1,0:T(1,128)S(1)}, u32[]{:S(2)}, u32[]{:S(2)}) async-start(f32[128,1,1]{2,1,0:T(1,128)} %broadcast_in_dim.44), calls=%async_computation | async-start | bytes 131072 | tf_op jit(solution)/shard_map/all_to_all | solution.py:68

commit v2 on v1

--- a/solution.py
+++ b/solution.py
@@ -65,7 +65,7 @@
 
 
 def grand_total(value, axes, size):
-    spread = lax.all_to_all(jnp.broadcast_to(value, (size, 1)), axes, 0, 0, tiled=True)
+    spread = lax.all_to_all(jnp.broadcast_to(value, (size,)), axes, 0, 0, tiled=True)
     return jnp.sum(spread)
 
 
@@ -144,8 +144,11 @@
         ]
         return jnp.concatenate(parts)
 
+    touched = {o for a, b, both in late_pairs for o in ((a, b) if both else (a,))}
     density = joined(0)
-    for offset in offsets[1:]:
+    for offset in [o for o in offsets[1:] if o not in touched]:
+        density = density + give_back(joined(offset), offset)
+    for offset in [o for o in offsets[1:] if o in touched]:
         density = density + give_back(joined(offset), offset)
 
     inverse = 1.0 / density.reshape(per_device, BLK)

time: 122 us -> 122 us (level)
  no operation moved by 1% of the time
where the time goes in v2:
time: 122 us; the launch traced here: 121 us
  starting transfers between devices  51.2 us (42%)
  waiting for transfers between devices  44.6 us (37%)
  matrix products  15.1 us (12%)
  other arithmetic  6.31 us (5%)
  local copies, waits for them, and re-layouts  2.8 us (2%)
  between operations  1.32 us (1%)
    ppermute x4, starting transfers between devices, give_back(): lax.ppermute(value, 'mem', [(ring[r], ring[(r + offset) % member_count])...  36.1 us
    ppermute x4, waiting for transfers between devices, fetch(): lax.ppermute(value, 'mem', [(ring[(r + offset) % member_count], ring[r])...  31.5 us
    dot_general x36, matrix products, kernel_sums(): lax.dot_general(left, right, (((1,), (1,)), ((), ())), preferred_element_...  15.1 us
    all_to_all x1, waiting for transfers between devices, grand_total(): lax.all_to_all(jnp.broadcast_to(value, (size,)), axes, 0, 0, tiled=True)  9.53 us
    all_to_all x1, starting transfers between devices, grand_total(): lax.all_to_all(jnp.broadcast_to(value, (size,)), axes, 0, 0, tiled=True)  8.1 us
    ppermute x4, starting transfers between devices, fetch(): lax.ppermute(value, 'mem', [(ring[(r + offset) % member_count], ring[r])...  6.98 us
    ppermute x4, waiting for transfers between devices, give_back(): lax.ppermute(value, 'mem', [(ring[r], ring[(r + offset) % member_count])...  3.57 us
  transfers between devices with their start and end apart: 9, of which 6 were waited for; matrix products, arithmetic and copies ran while one was open for 4% of the time, Pallas kernels for 0%

profile of v2, /device:TPU:0, one launch (start us, length us, event | category | flops | bytes accessed | tf_op | source)
XLA Modules:
  0.0 121.2 jit_solution(17659979876329351026)
XLA Ops:
  0.0 0.8 fusion.144
  0.9 0.7 compare_and_fusion
  1.7 0.6 gather_fusion
  2.6 2.1 %collective-permute-start.4 = (bf16[1024,768]{1,0:T(8,128)(2,1)S(1)}, bf16[1024,768]{1,0:T(8,128)(2,1)S(1)}, u32[]{:S(2)}, u32[]{:S(2)}) collective-permute-start(bf16[1024,768]{1,0:T(8,128)(2,1)S(1)} %bitcast_select_fusion), channel_id=1, source_target_pairs={{9,0},{0,2},{2,4},{4,6},{6,14},{14,12},{12,10},{10,8},{8,1},{1,3},... | collective-permute-start | bytes 4718600 | tf_op jit(solution)/shard_map/ppermute | solution.py:97
  4.7 3.7 %collective-permute-start.1 = (bf16[1024,768]{1,0:T(8,128)(2,1)S(1)}, bf16[1024,768]{1,0:T(8,128)(2,1)S(1)}, u32[]{:S(2)}, u32[]{:S(2)}) collective-permute-start(bf16[1024,768]{1,0:T(8,128)(2,1)S(1)} %bitcast_select_fusion), channel_id=1, source_target_pairs={{12,0},{10,2},{8,4},{1,6},{3,14},{5,12},{7,10},{15,8},{13,1},{11,3... | collective-permute-start | bytes 4718600 | tf_op jit(solution)/shard_map/ppermute | solution.py:97
  8.5 1.2 collective-permute-start
  9.6 0.6 multiply_reduce_fusion.4
  11.3 0.7 fusion.3
  12.0 27.2 %collective-permute-done.4 = bf16[1024,768]{1,0:T(8,128)(2,1)S(1)} collective-permute-done((bf16[1024,768]{1,0:T(8,128)(2,1)S(1)}, bf16[1024,768]{1,0:T(8,128)(2,1)S(1)}, u32[]{:S(2)}, u32[]{:S(2)}) %collective-permute-start.4) | collective-permute-done | bytes 1572896 | tf_op jit(solution)/shard_map/ppermute | solution.py:97
  40.1 4.0 %collective-permute-done.1 = bf16[1024,768]{1,0:T(8,128)(2,1)S(1)} collective-permute-done((bf16[1024,768]{1,0:T(8,128)(2,1)S(1)}, bf16[1024,768]{1,0:T(8,128)(2,1)S(1)}, u32[]{:S(2)}, u32[]{:S(2)}) %collective-permute-start.1) | collective-permute-done | bytes 1572896 | tf_op jit(solution)/shard_map/ppermute | solution.py:97
  45.2 0.4 fusion.150
  49.5 0.6 convolution_multiply_fusion.2
  50.1 0.6 convolution_multiply_fusion
  50.7 0.6 convolution_multiply_fusion.6
  51.3 0.6 convolution_multiply_fusion.4
  51.9 0.6 convolution_multiply_fusion.3
  52.6 0.6 convolution_multiply_fusion.7
  53.2 2.1 %fusion.27 = (f32[512]{0:T(512)S(1)}, f32[512]{0:T(512)S(1)}, f32[512]{0:T(512)S(1)}, f32[512]{0:T(512)S(1)}, f32[512]{0:T(512)S(1)}, /*index=5*/f32[512]{0:T(51...) fusion(f32[512]{0:T(512)S(1)} %slice-done, ...), kind=kOutput, calls=%fused_computation.80 | convolution fusion | flops 412083200 | bytes 7907328 | tf_op jit(solution)/shard_map/dot_general | solution.py:73
  55.3 0.4 fusion.153
  56.2 0.7 exponential_reduce_fusion
  57.3 0.4 fusion.152
  59.1 30.6 %collective-permute-start.5 = (f32[1024]{0:T(1024)S(1)}, f32[1024]{0:T(1024)S(1)}, u32[]{:S(2)}, u32[]{:S(2)}) collective-permute-start(f32[1024]{0:T(1024)S(1)} %pad_maximum_fusion.1), channel_id=1, source_target_pairs={{0,2},{2,4},{4,6},{6,14},{14,12},{12,10},{10,8},{8,1},{1,3},{3,5},... | collective-permute-start | bytes 12296 | tf_op jit(solution)/shard_map/ppermute | solution.py:104
  90.2 5.1 %collective-permute-start.6 = (f32[1024]{0:T(1024)S(1)}, f32[1024]{0:T(1024)S(1)}, u32[]{:S(2)}, u32[]{:S(2)}) collective-permute-start(f32[1024]{0:T(1024)S(1)} %pad_maximum_fusion.2), channel_id=1, source_target_pairs={{0,12},{2,10},{4,8},{6,1},{14,3},{12,5},{10,7},{8,15},{1,13},{3,11... | collective-permute-start | bytes 12296 | tf_op jit(solution)/shard_map/ppermute | solution.py:104
  95.4 1.2 collective-permute-done.6
  96.6 2.4 %collective-permute-done.7 = f32[1024]{0:T(1024)S(1)} collective-permute-done((f32[1024]{0:T(1024)S(1)}, f32[1024]{0:T(1024)S(1)}, u32[]{:S(2)}, u32[]{:S(2)}) %collective-permute-start.7) | collective-permute-done | bytes 4128 | tf_op jit(solution)/shard_map/ppermute | solution.py:104
  99.0 0.6 fusion.154
  99.6 1.3 %broadcast_in_dim.44 = f32[128,1,1]{2,1,0:T(1,128)} broadcast(f32[]{:T(128)} %get-tuple-element.129), dimensions={} | broadcast | bytes 516 | tf_op jit(solution)/shard_map/broadcast_in_dim | solution.py:68
  100.9 8.1 %all-to-all-start = ((f32[128,1,1]{2,1,0:T(1,128)}), f32[128,1,1]{2,1,0:T(1,128)S(1)}, u32[]{:S(2)}, u32[]{:S(2)}) async-start(f32[128,1,1]{2,1,0:T(1,128)} %broadcast_in_dim.44), calls=%async_computation | async-start | bytes 131072 | tf_op jit(solution)/shard_map/all_to_all | solution.py:68
  109.0 9.5 %all-to-all-done = f32[128,1,1]{2,1,0:T(1,128)S(1)} async-done(((f32[128,1,1]{2,1,0:T(1,128)}), f32[128,1,1]{2,1,0:T(1,128)S(1)}, u32[]{:S(2)}, u32[]{:S(2)}) %all-to-all-start) | async-done | bytes 544 | tf_op jit(solution)/shard_map/all_to_all | solution.py:68
  118.5 0.7 reduce_sum.721
  120.0 0.6 gather_fusion.1
  120.5 0.7 select_bitcast_fusion
  (98 shorter events, 9.7 us)
Async XLA Ops:
  0.0 1.7 %copy-start = (bf16[1024,768]{1,0:T(8,128)(2,1)S(1)}, bf16[1024,768]{1,0:T(8,128)(2,1)}, u32[]{:S(2)}) copy-start(bf16[1024,768]{1,0:T(8,128)(2,1)} %param.2) | copy-start | bytes 4718596
  2.6 36.6 %collective-permute-start.4 = (bf16[1024,768]{1,0:T(8,128)(2,1)S(1)}, bf16[1024,768]{1,0:T(8,128)(2,1)S(1)}, u32[]{:S(2)}, u32[]{:S(2)}) collective-permute-start(bf16[1024,768]{1,0:T(8,128)(2,1)S(1)} %bitcast_select_fusion), channel_id=1, source_target_pairs={{9,0},{0,2},{2,4},{4,6},{6,14},{14,12},{12,10},{10,8},{8,1},{1,3},... | collective-permute-start | bytes 4718600 | tf_op jit(solution)/shard_map/ppermute | solution.py:97
  4.7 34.9 %collective-permute-start.2 = (bf16[1024,768]{1,0:T(8,128)(2,1)S(1)}, bf16[1024,768]{1,0:T(8,128)(2,1)S(1)}, u32[]{:S(2)}, u32[]{:S(2)}) collective-permute-start(bf16[1024,768]{1,0:T(8,128)(2,1)S(1)} %bitcast_select_fusion), channel_id=1, source_target_pairs={{1,0},{3,2},{5,4},{7,6},{15,14},{13,12},{11,10},{9,8},{0,1},{2,3},... | collective-permute-start | bytes 4718600 | tf_op jit(solution)/shard_map/ppermute | solution.py:97
  4.7 39.3 %collective-permute-start.1 = (bf16[1024,768]{1,0:T(8,128)(2,1)S(1)}, bf16[1024,768]{1,0:T(8,128)(2,1)S(1)}, u32[]{:S(2)}, u32[]{:S(2)}) collective-permute-start(bf16[1024,768]{1,0:T(8,128)(2,1)S(1)} %bitcast_select_fusion), channel_id=1, source_target_pairs={{12,0},{10,2},{8,4},{1,6},{3,14},{5,12},{7,10},{15,8},{13,1},{11,3... | collective-permute-start | bytes 4718600 | tf_op jit(solution)/shard_map/ppermute | solution.py:97
  8.5 36.3 %collective-permute-start = (bf16[1024,768]{1,0:T(8,128)(2,1)S(1)}, bf16[1024,768]{1,0:T(8,128)(2,1)S(1)}, u32[]{:S(2)}, u32[]{:S(2)}) collective-permute-start(bf16[1024,768]{1,0:T(8,128)(2,1)S(1)} %bitcast_select_fusion), channel_id=1, source_target_pairs={{2,0},{4,2},{6,4},{14,6},{12,14},{10,12},{8,10},{1,8},{3,1},{5,3},... | collective-permute-start | bytes 4718600 | tf_op jit(solution)/shard_map/ppermute | solution.py:97
  39.6 4.8 %copy-start.1 = (f32[1024]{0:T(1024)}, f32[1024]{0:T(1024)S(1)}, u32[]{:S(2)}) copy-start(f32[1024]{0:T(1024)S(1)} %multiply_reduce_fusion) | copy-start | bytes 12292
  44.4 1.2 copy-start.2
  45.1 0.9 copy-start.3
  52.5 0.7 slice-start
  52.5 0.7 slice-start.1
  52.5 0.7 slice-start.2
  58.3 37.1 %collective-permute-start.3 = (f32[1024]{0:T(1024)S(1)}, f32[1024]{0:T(1024)S(1)}, u32[]{:S(2)}, u32[]{:S(2)}) collective-permute-start(f32[1024]{0:T(1024)S(1)} %pad_maximum_fusion), channel_id=1, source_target_pairs={{0,1},{2,3},{4,5},{6,7},{14,15},{12,13},{10,11},{8,9},{1,0},{3,2},... | collective-permute-start | bytes 12296 | tf_op jit(solution)/shard_map/ppermute | solution.py:104
  59.1 36.3 %collective-permute-start.5 = (f32[1024]{0:T(1024)S(1)}, f32[1024]{0:T(1024)S(1)}, u32[]{:S(2)}, u32[]{:S(2)}) collective-permute-start(f32[1024]{0:T(1024)S(1)} %pad_maximum_fusion.1), channel_id=1, source_target_pairs={{0,2},{2,4},{4,6},{6,14},{14,12},{12,10},{10,8},{8,1},{1,3},{3,5},... | collective-permute-start | bytes 12296 | tf_op jit(solution)/shard_map/ppermute | solution.py:104
  90.2 6.4 %collective-permute-start.6 = (f32[1024]{0:T(1024)S(1)}, f32[1024]{0:T(1024)S(1)}, u32[]{:S(2)}, u32[]{:S(2)}) collective-permute-start(f32[1024]{0:T(1024)S(1)} %pad_maximum_fusion.2), channel_id=1, source_target_pairs={{0,12},{2,10},{4,8},{6,1},{14,3},{12,5},{10,7},{8,15},{1,13},{3,11... | collective-permute-start | bytes 12296 | tf_op jit(solution)/shard_map/ppermute | solution.py:104
  95.3 3.7 %collective-permute-start.7 = (f32[1024]{0:T(1024)S(1)}, f32[1024]{0:T(1024)S(1)}, u32[]{:S(2)}, u32[]{:S(2)}) collective-permute-start(f32[1024]{0:T(1024)S(1)} %pad_maximum_fusion.3), channel_id=1, source_target_pairs={{0,9},{2,0},{4,2},{6,4},{14,6},{12,14},{10,12},{8,10},{1,8},{3,1},... | collective-permute-start | bytes 12296 | tf_op jit(solution)/shard_map/ppermute | solution.py:104
  100.9 17.7 %all-to-all-start = ((f32[128,1,1]{2,1,0:T(1,128)}), f32[128,1,1]{2,1,0:T(1,128)S(1)}, u32[]{:S(2)}, u32[]{:S(2)}) async-start(f32[128,1,1]{2,1,0:T(1,128)} %broadcast_in_dim.44), calls=%async_computation | async-start | bytes 131072 | tf_op jit(solution)/shard_map/all_to_all | solution.py:68

commit v3 on v2

--- a/solution.py
+++ b/solution.py
@@ -122,15 +122,29 @@
         for offset in {o for a, b, _ in chosen for o in (a, b)} | {0}:
             if offset not in norms:
                 norms[offset] = squared(held[offset])
+        groups = {}
+        for a, b, both in chosen:
+            groups.setdefault((a, both), []).append(b)
         for index, (start, end) in enumerate(spans):
-            for a, b, both in chosen:
+            for (a, both), others in groups.items():
+                if not both:
+                    for b in others:
+                        rows, _ = kernel_sums(
+                            held[a][start:end], held[b][start:end],
+                            norms[a][start:end], norms[b][start:end], False,
+                        )
+                        add(a, index, rows)
+                    continue
                 rows, cols = kernel_sums(
-                    held[a][start:end], held[b][start:end],
-                    norms[a][start:end], norms[b][start:end], both,
+                    held[a][start:end],
+                    jnp.concatenate([held[b][start:end] for b in others]),
+                    norms[a][start:end],
+                    jnp.concatenate([norms[b][start:end] for b in others]),
+                    True,
                 )
                 add(a, index, rows)
-                if both:
-                    add(b, index, cols)
+                for slot, b in enumerate(others):
+                    add(b, index, cols[slot * (end - start):(slot + 1) * (end - start)])
 
     late_pairs = [p for p in pairs if late in p[:2]]
     blocks([(0, 0, False)] + [p for p in pairs if late not in p[:2]])
@@ -154,12 +168,12 @@
     inverse = 1.0 / density.reshape(per_device, BLK)
     total = grand_total(jnp.sum(inverse), ("clu", "mem"), lax.axis_size("clu") * member_count)
     everything = jnp.float32(row_count * lax.axis_size("clu") * member_count)
-    weight = inverse * (everything / total)
     spots = jnp.arange(per_device, dtype=jnp.int32)
     back = jnp.sum(
         jnp.where(order[None, :] == spots[:, None], spots[None, :], 0), axis=1
     )
-    return jnp.take(weight, back, axis=0).reshape(-1)
+    stored = jnp.take(inverse, back, axis=0).reshape(-1)
+    return stored * (everything / total)
 
 
 def solution(mesh):

time: 122 us -> 120 us (0.984)
  waiting for transfers between devices: 44.6 us -> 75.2 us
  starting transfers between devices: 51.2 us -> 20.7 us
  matrix products: 15.1 us -> 13.1 us
    ppermute x4, waiting for transfers between devices: 31.5 us -> 63.4 us  [fetch(): lax.ppermute(value, 'mem', [(ring[(r + offset) % member_count], ring[r])...]
    ppermute x4, starting transfers between devices: 36.1 us -> 4.92 us  [give_back(): lax.ppermute(value, 'mem', [(ring[r], ring[(r + offset) % member_count])...]
    dot_general x36 -> x24, matrix products: 15.1 us -> 13.1 us  [kernel_sums(): lax.dot_general(left, right, (((1,), (1,)), ((), ())), preferred_element_...]
    all_to_all x1, starting transfers between devices: 8.1 us -> 9.45 us  [grand_total(): lax.all_to_all(jnp.broadcast_to(value, (size,)), axes, 0, 0, tiled=True)]
  transfers between devices with their start and end apart: 9 -> 9, of which waited for: 6 -> 6; matrix products, arithmetic and copies ran while one was open for 4% -> 6% of each run, Pallas kernels for 0% -> 0%
where the time goes in v3:
time: 120 us; the launch traced here: 119 us
  waiting for transfers between devices  75.2 us (63%)
  starting transfers between devices  20.7 us (17%)
  matrix products  13.1 us (11%)
  other arithmetic  6.27 us (5%)
  local copies, waits for them, and re-layouts  3.05 us (3%)
    ppermute x4, waiting for transfers between devices, fetch(): lax.ppermute(value, 'mem', [(ring[(r + offset) % member_count], ring[r])...  63.4 us
    dot_general x24, matrix products, kernel_sums(): lax.dot_general(left, right, (((1,), (1,)), ((), ())), preferred_element_...  13.1 us
    all_to_all x1, starting transfers between devices, grand_total(): lax.all_to_all(jnp.broadcast_to(value, (size,)), axes, 0, 0, tiled=True)  9.45 us
    all_to_all x1, waiting for transfers between devices, grand_total(): lax.all_to_all(jnp.broadcast_to(value, (size,)), axes, 0, 0, tiled=True)  8.97 us
    ppermute x4, starting transfers between devices, fetch(): lax.ppermute(value, 'mem', [(ring[(r + offset) % member_count], ring[r])...  6.38 us
    ppermute x4, starting transfers between devices, give_back(): lax.ppermute(value, 'mem', [(ring[r], ring[(r + offset) % member_count])...  4.92 us
    ppermute x4, waiting for transfers between devices, give_back(): lax.ppermute(value, 'mem', [(ring[r], ring[(r + offset) % member_count])...  2.88 us
  transfers between devices with their start and end apart: 9, of which 6 were waited for; matrix products, arithmetic and copies ran while one was open for 6% of the time, Pallas kernels for 0%

profile of v3, /device:TPU:0, one launch (start us, length us, event | category | flops | bytes accessed | tf_op | source)
XLA Modules:
  0.0 119.5 jit_solution(10879208892177091091)
XLA Ops:
  0.0 0.9 compare_and_fusion
  0.9 0.7 fusion.63
  1.7 0.6 gather_fusion
  2.7 1.7 %collective-permute-start.1 = (bf16[1024,768]{1,0:T(8,128)(2,1)S(1)}, bf16[1024,768]{1,0:T(8,128)(2,1)S(1)}, u32[]{:S(2)}, u32[]{:S(2)}) collective-permute-start(bf16[1024,768]{1,0:T(8,128)(2,1)S(1)} %bitcast_select_fusion), channel_id=1, source_target_pairs={{2,0},{4,2},{6,4},{14,6},{12,14},{10,12},{8,10},{1,8},{3,1},{5,3},... | collective-permute-start | bytes 4718600 | tf_op jit(solution)/shard_map/ppermute | solution.py:97
  4.4 2.7 %collective-permute-start.2 = (bf16[1024,768]{1,0:T(8,128)(2,1)S(1)}, bf16[1024,768]{1,0:T(8,128)(2,1)S(1)}, u32[]{:S(2)}, u32[]{:S(2)}) collective-permute-start(bf16[1024,768]{1,0:T(8,128)(2,1)S(1)} %bitcast_select_fusion), channel_id=1, source_target_pairs={{12,0},{10,2},{8,4},{1,6},{3,14},{5,12},{7,10},{15,8},{13,1},{11,3... | collective-permute-start | bytes 4718600 | tf_op jit(solution)/shard_map/ppermute | solution.py:97
  7.1 1.9 %collective-permute-start.4 = (bf16[1024,768]{1,0:T(8,128)(2,1)S(1)}, bf16[1024,768]{1,0:T(8,128)(2,1)S(1)}, u32[]{:S(2)}, u32[]{:S(2)}) collective-permute-start(bf16[1024,768]{1,0:T(8,128)(2,1)S(1)} %bitcast_select_fusion), channel_id=1, source_target_pairs={{9,0},{0,2},{2,4},{4,6},{6,14},{14,12},{12,10},{10,8},{8,1},{1,3},... | collective-permute-start | bytes 4718600 | tf_op jit(solution)/shard_map/ppermute | solution.py:97
  9.0 0.6 multiply_reduce_fusion.4
  10.7 0.7 fusion.6
  11.9 28.0 %collective-permute-done.1 = bf16[1024,768]{1,0:T(8,128)(2,1)S(1)} collective-permute-done((bf16[1024,768]{1,0:T(8,128)(2,1)S(1)}, bf16[1024,768]{1,0:T(8,128)(2,1)S(1)}, u32[]{:S(2)}, u32[]{:S(2)}) %collective-permute-start.1) | collective-permute-done | bytes 1572896 | tf_op jit(solution)/shard_map/ppermute | solution.py:97
  40.2 3.9 %collective-permute-done.2 = bf16[1024,768]{1,0:T(8,128)(2,1)S(1)} collective-permute-done((bf16[1024,768]{1,0:T(8,128)(2,1)S(1)}, bf16[1024,768]{1,0:T(8,128)(2,1)S(1)}, u32[]{:S(2)}, u32[]{:S(2)}) %collective-permute-start.2) | collective-permute-done | bytes 1572896 | tf_op jit(solution)/shard_map/ppermute | solution.py:97
  44.6 31.5 %collective-permute-done.4 = bf16[1024,768]{1,0:T(8,128)(2,1)S(1)} collective-permute-done((bf16[1024,768]{1,0:T(8,128)(2,1)S(1)}, bf16[1024,768]{1,0:T(8,128)(2,1)S(1)}, u32[]{:S(2)}, u32[]{:S(2)}) %collective-permute-start.4) | collective-permute-done | bytes 1572896 | tf_op jit(solution)/shard_map/ppermute | solution.py:97
  78.0 0.5 fusion.98
  78.7 1.3 %fusion.96 = (f32[1024]{0:T(1024)S(1)}, f32[512]{0:T(512)S(1)}) fusion(bf16[512,768]{1,0:T(8,128)(2,1)S(1)} %bitcast.57, bf16[512,768]{1,0:T(8,128)(2,1)S(1)} %slice.363, bf16[512,768]{1,0:T(8,128)(2,1)S(1)} %slice.362, f32[1024]{0:T(1024)S(1)} %get-tuple-element.102, f32[512]{0:T(512)S(1)} %slice_bitcast_fusion.12), kind=kOutput, calls=%fused_computation.203 | convolution fusion | flops 811596288 | bytes 2371584 | tf_op jit(solution)/shard_map/dot_general | solution.py:73
  82.3 0.6 fusion.34
  83.0 0.8 fusion.28
  83.8 0.7 exponential_reduce_fusion
  84.5 1.3 %fusion.95 = (f32[1024]{0:T(1024)S(1)}, f32[512]{0:T(512)S(1)}) fusion(bf16[512,768]{1,0:T(8,128)(2,1)S(1)} %slice.361, bf16[512,768]{1,0:T(8,128)(2,1)S(1)} %slice.363, bf16[1024,768]{1,0:T(8,128)(2,1)S(1)} %collective-permute-done.1, f32[1024]{0:T(1024)S(1)} %get-tuple-element.101, f32[512]{0:T(512)S(1)} %slice.293), kind=kOutput, calls=%fused_computation.202 | convolution fusion | flops 811596288 | bytes 2371584 | tf_op jit(solution)/shard_map/dot_general | solution.py:73
  85.9 0.7 collective-permute-start.3
  86.6 1.3 %fusion.94 = (f32[1024]{0:T(1024)S(1)}, f32[512]{0:T(512)S(1)}) fusion(bf16[512,768]{1,0:T(8,128)(2,1)S(1)} %slice.363, bf16[512,768]{1,0:T(8,128)(2,1)S(1)} %slice.362, bf16[1024,768]{1,0:T(8,128)(2,1)S(1)} %collective-permute-done.4, f32[1024]{0:T(1024)S(1)} %get-tuple-element.102, f32[512]{0:T(512)S(1)} %slice-done), kind=kOutput, calls=%fused_computation.201 | convolution fusion | flops 811596288 | bytes 2371584 | tf_op jit(solution)/shard_map/dot_general | solution.py:73
  87.9 0.5 fusion.97
  89.3 1.7 %collective-permute-start.5 = (f32[1024]{0:T(1024)S(1)}, f32[1024]{0:T(1024)S(1)}, u32[]{:S(2)}, u32[]{:S(2)}) collective-permute-start(f32[1024]{0:T(1024)S(1)} %pad_maximum_fusion.17), channel_id=1, source_target_pairs={{0,2},{2,4},{4,6},{6,14},{14,12},{12,10},{10,8},{8,1},{1,3},{3,5},... | collective-permute-start | bytes 12296 | tf_op jit(solution)/shard_map/ppermute | solution.py:104
  91.1 1.8 %collective-permute-start.6 = (f32[1024]{0:T(1024)S(1)}, f32[1024]{0:T(1024)S(1)}, u32[]{:S(2)}, u32[]{:S(2)}) collective-permute-start(f32[1024]{0:T(1024)S(1)} %pad_maximum_fusion.18), channel_id=1, source_target_pairs={{0,12},{2,10},{4,8},{6,1},{14,3},{12,5},{10,7},{8,15},{1,13},{3,11... | collective-permute-start | bytes 12296 | tf_op jit(solution)/shard_map/ppermute | solution.py:104
  92.8 0.7 collective-permute-start.7
  93.6 1.7 %collective-permute-done.6 = f32[1024]{0:T(1024)S(1)} collective-permute-done((f32[1024]{0:T(1024)S(1)}, f32[1024]{0:T(1024)S(1)}, u32[]{:S(2)}, u32[]{:S(2)}) %collective-permute-start.6) | collective-permute-done | bytes 4128 | tf_op jit(solution)/shard_map/ppermute | solution.py:104
  95.3 1.1 collective-permute-done.7
  96.5 0.6 fusion.101
  97.1 1.3 %broadcast_in_dim.45 = f32[128,1,1]{2,1,0:T(1,128)} broadcast(f32[]{:T(128)} %get-tuple-element.69), dimensions={} | broadcast | bytes 516 | tf_op jit(solution)/shard_map/broadcast_in_dim | solution.py:68
  98.4 9.4 %all-to-all-start = ((f32[128,1,1]{2,1,0:T(1,128)}), f32[128,1,1]{2,1,0:T(1,128)S(1)}, u32[]{:S(2)}, u32[]{:S(2)}) async-start(f32[128,1,1]{2,1,0:T(1,128)} %broadcast_in_dim.45), calls=%async_computation | async-start | bytes 131072 | tf_op jit(solution)/shard_map/all_to_all | solution.py:68
  107.8 0.6 gather_fusion.1
  108.4 9.0 %all-to-all-done = f32[128,1,1]{2,1,0:T(1,128)S(1)} async-done(((f32[128,1,1]{2,1,0:T(1,128)}), f32[128,1,1]{2,1,0:T(1,128)S(1)}, u32[]{:S(2)}, u32[]{:S(2)}) %all-to-all-start) | async-done | bytes 544 | tf_op jit(solution)/shard_map/all_to_all | solution.py:68
  117.4 0.7 reduce_sum.482
  118.8 0.7 multiply_bitcast_fusion
  (78 shorter events, 7.9 us)
Async XLA Ops:
  0.0 1.7 %copy-start = (bf16[1024,768]{1,0:T(8,128)(2,1)S(1)}, bf16[1024,768]{1,0:T(8,128)(2,1)}, u32[]{:S(2)}) copy-start(bf16[1024,768]{1,0:T(8,128)(2,1)} %param.2) | copy-start | bytes 4718596
  2.6 8.8 %collective-permute-start = (bf16[1024,768]{1,0:T(8,128)(2,1)S(1)}, bf16[1024,768]{1,0:T(8,128)(2,1)S(1)}, u32[]{:S(2)}, u32[]{:S(2)}) collective-permute-start(bf16[1024,768]{1,0:T(8,128)(2,1)S(1)} %bitcast_select_fusion), channel_id=1, source_target_pairs={{1,0},{3,2},{5,4},{7,6},{15,14},{13,12},{11,10},{9,8},{0,1},{2,3},... | collective-permute-start | bytes 4718600 | tf_op jit(solution)/shard_map/ppermute | solution.py:97
  2.7 37.1 %collective-permute-start.1 = (bf16[1024,768]{1,0:T(8,128)(2,1)S(1)}, bf16[1024,768]{1,0:T(8,128)(2,1)S(1)}, u32[]{:S(2)}, u32[]{:S(2)}) collective-permute-start(bf16[1024,768]{1,0:T(8,128)(2,1)S(1)} %bitcast_select_fusion), channel_id=1, source_target_pairs={{2,0},{4,2},{6,4},{14,6},{12,14},{10,12},{8,10},{1,8},{3,1},{5,3},... | collective-permute-start | bytes 4718600 | tf_op jit(solution)/shard_map/ppermute | solution.py:97
  4.4 39.7 %collective-permute-start.2 = (bf16[1024,768]{1,0:T(8,128)(2,1)S(1)}, bf16[1024,768]{1,0:T(8,128)(2,1)S(1)}, u32[]{:S(2)}, u32[]{:S(2)}) collective-permute-start(bf16[1024,768]{1,0:T(8,128)(2,1)S(1)} %bitcast_select_fusion), channel_id=1, source_target_pairs={{12,0},{10,2},{8,4},{1,6},{3,14},{5,12},{7,10},{15,8},{13,1},{11,3... | collective-permute-start | bytes 4718600 | tf_op jit(solution)/shard_map/ppermute | solution.py:97
  7.1 69.0 %collective-permute-start.4 = (bf16[1024,768]{1,0:T(8,128)(2,1)S(1)}, bf16[1024,768]{1,0:T(8,128)(2,1)S(1)}, u32[]{:S(2)}, u32[]{:S(2)}) collective-permute-start(bf16[1024,768]{1,0:T(8,128)(2,1)S(1)} %bitcast_select_fusion), channel_id=1, source_target_pairs={{9,0},{0,2},{2,4},{4,6},{6,14},{14,12},{12,10},{10,8},{8,1},{1,3},... | collective-permute-start | bytes 4718600 | tf_op jit(solution)/shard_map/ppermute | solution.py:97
  76.4 0.9 copy-start.1
  84.5 2.1 %slice-start = ((f32[1024]{0:T(1024)}), f32[512]{0:T(512)S(1)}, s32[]{:S(2)}) async-start(f32[1024]{0:T(1024)} %copy-done.1), calls=%async_computation.1 | async-start | bytes 4096 | tf_op jit(solution)/shard_map/slice | solution.py:141
  85.9 7.7 %collective-permute-start.3 = (f32[1024]{0:T(1024)S(1)}, f32[1024]{0:T(1024)S(1)}, u32[]{:S(2)}, u32[]{:S(2)}) collective-permute-start(f32[1024]{0:T(1024)S(1)} %pad_maximum_fusion.16), channel_id=1, source_target_pairs={{0,1},{2,3},{4,5},{6,7},{14,15},{12,13},{10,11},{8,9},{1,0},{3,2},... | collective-permute-start | bytes 12296 | tf_op jit(solution)/shard_map/ppermute | solution.py:104
  89.3 4.2 %collective-permute-start.5 = (f32[1024]{0:T(1024)S(1)}, f32[1024]{0:T(1024)S(1)}, u32[]{:S(2)}, u32[]{:S(2)}) collective-permute-start(f32[1024]{0:T(1024)S(1)} %pad_maximum_fusion.17), channel_id=1, source_target_pairs={{0,2},{2,4},{4,6},{6,14},{14,12},{12,10},{10,8},{8,1},{1,3},{3,5},... | collective-permute-start | bytes 12296 | tf_op jit(solution)/shard_map/ppermute | solution.py:104
  91.1 4.2 %collective-permute-start.6 = (f32[1024]{0:T(1024)S(1)}, f32[1024]{0:T(1024)S(1)}, u32[]{:S(2)}, u32[]{:S(2)}) collective-permute-start(f32[1024]{0:T(1024)S(1)} %pad_maximum_fusion.18), channel_id=1, source_target_pairs={{0,12},{2,10},{4,8},{6,1},{14,3},{12,5},{10,7},{8,15},{1,13},{3,11... | collective-permute-start | bytes 12296 | tf_op jit(solution)/shard_map/ppermute | solution.py:104
  92.8 3.6 %collective-permute-start.7 = (f32[1024]{0:T(1024)S(1)}, f32[1024]{0:T(1024)S(1)}, u32[]{:S(2)}, u32[]{:S(2)}) collective-permute-start(f32[1024]{0:T(1024)S(1)} %pad_maximum_fusion.19), channel_id=1, source_target_pairs={{0,9},{2,0},{4,2},{6,4},{14,6},{12,14},{10,12},{8,10},{1,8},{3,1},... | collective-permute-start | bytes 12296 | tf_op jit(solution)/shard_map/ppermute | solution.py:104
  98.4 19.0 %all-to-all-start = ((f32[128,1,1]{2,1,0:T(1,128)}), f32[128,1,1]{2,1,0:T(1,128)S(1)}, u32[]{:S(2)}, u32[]{:S(2)}) async-start(f32[128,1,1]{2,1,0:T(1,128)} %broadcast_in_dim.45), calls=%async_computation | async-start | bytes 131072 | tf_op jit(solution)/shard_map/all_to_all | solution.py:68

commit v4 on v3

--- a/solution.py
+++ b/solution.py
@@ -108,9 +108,17 @@
         )
 
     late = offsets[-1]
+    first = 5 if member_count == 16 else None
     held = {0: ordered}
     for offset in offsets[1:]:
-        held[offset] = fetch(ordered, offset)
+        held[offset] = fetch(embeddings if offset == first else ordered, offset)
+    if first is not None:
+        spot = jnp.array([ring.index(m) for m in range(member_count)], jnp.int32)[position]
+        sender = jnp.array(ring, jnp.int32)[(spot + first) % member_count]
+        sender_order = lax.dynamic_slice_in_dim(block_order[0], sender * per_device, per_device)
+        held[first] = jnp.take(
+            held[first].reshape(per_device, BLK, width), sender_order, axis=0
+        ).reshape(row_count, width)
     norms = {}
     partial = {offset: [None] * len(spans) for offset in offsets}
 

time: 120 us -> 127 us (1.058)
  waiting for transfers between devices: 75.2 us -> 52.7 us
  matrix products: 13.1 us -> 25.4 us
  local copies, waits for them, and re-layouts: 3.05 us -> 14.2 us
  other arithmetic: 6.27 us -> 11 us
  between operations: 1.1 us -> 2.56 us
    ppermute x4, waiting for transfers between devices: 63.4 us -> 40.2 us  [fetch(): lax.ppermute(value, 'mem', [(ring[(r + offset) % member_count], ring[r])...]
    dot_general x24, matrix products: 13.1 us -> 25.4 us  [kernel_sums(): lax.dot_general(left, right, (((1,), (1,)), ((), ())), preferred_element_...]
    reduce_sum x5, other arithmetic: 2.09 us -> 6.2 us  [squared(): return jnp.sum(jnp.square(values.astype(jnp.float32)), axis=1)]
    gather x0 -> x1, local copies, waits for them, and re-layouts: none -> 3.35 us  [shards(): jnp.take(held[first].reshape(per_device, BLK, width), sender_order, axis=0)]
    dynamic_slice x0 -> x2, local copies, waits for them, and re-layouts: none -> 2.48 us  [the longest x1 1.24 us: shards(): sender = jnp.array(ring, jnp.int32)[(spot + first) % member_count]]
    slice x2, local copies, waits for them, and re-layouts: 0.08 us -> 2.21 us  [blocks(): held[a][start:end]]
    gather x1, local copies, waits for them, and re-layouts: 0.65 us -> 2.06 us  [shards(): ordered = jnp.take(blocks, order, axis=0).reshape(row_count, width)]
  transfers between devices with their start and end apart: 9 -> 9, of which waited for: 6 -> 5; matrix products, arithmetic and copies ran while one was open for 6% -> 25% of each run, Pallas kernels for 0% -> 0%
where the time goes in v4:
time: 127 us; the launch traced here: 126 us
  waiting for transfers between devices  52.7 us (41%)
  matrix products  25.4 us (20%)
  starting transfers between devices  20.5 us (16%)
  local copies, waits for them, and re-layouts  14.2 us (11%)
  other arithmetic  11 us (9%)
  between operations  2.56 us (2%)
    ppermute x4, waiting for transfers between devices, fetch(): lax.ppermute(value, 'mem', [(ring[(r + offset) % member_count], ring[r])...  40.2 us
    dot_general x24, matrix products, kernel_sums(): lax.dot_general(left, right, (((1,), (1,)), ((), ())), preferred_element_...  25.4 us
    all_to_all x1, waiting for transfers between devices, grand_total(): lax.all_to_all(jnp.broadcast_to(value, (size,)), axes, 0, 0, tiled=True)  8.96 us
    all_to_all x1, starting transfers between devices, grand_total(): lax.all_to_all(jnp.broadcast_to(value, (size,)), axes, 0, 0, tiled=True)  8.21 us
    ppermute x4, starting transfers between devices, fetch(): lax.ppermute(value, 'mem', [(ring[(r + offset) % member_count], ring[r])...  6.29 us
    reduce_sum x5, other arithmetic, squared(): return jnp.sum(jnp.square(values.astype(jnp.float32)), axis=1)  6.2 us
    ppermute x4, starting transfers between devices, give_back(): lax.ppermute(value, 'mem', [(ring[r], ring[(r + offset) % member_count])...  5.96 us
    ppermute x4, waiting for transfers between devices, give_back(): lax.ppermute(value, 'mem', [(ring[r], ring[(r + offset) % member_count])...  3.56 us
  transfers between devices with their start and end apart: 9, of which 5 were waited for; matrix products, arithmetic and copies ran while one was open for 25% of the time, Pallas kernels for 0%

profile of v4, /device:TPU:0, one launch (start us, length us, event | category | flops | bytes accessed | tf_op | source)
XLA Modules:
  0.0 126.2 jit_solution(9261868336885538163)
XLA Ops:
  0.0 3.6 %collective-permute-start.2 = (bf16[1024,768]{1,0:T(8,128)(2,1)}, bf16[1024,768]{1,0:T(8,128)(2,1)}, u32[]{:S(2)}, u32[]{:S(2)}) collective-permute-start(bf16[1024,768]{1,0:T(8,128)(2,1)} %param.6), channel_id=1, source_target_pairs={{12,0},{10,2},{8,4},{1,6},{3,14},{5,12},{7,10},{15,8},{13,1},{11,3... | collective-permute-start | bytes 4718600 | tf_op jit(solution)/shard_map/ppermute | solution.py:97
  3.6 1.2 dynamic_slice.15
  5.5 1.2 dynamic_slice.16
  7.4 1.3 %compare_and_fusion.1 = (pred[8]{0:T(512)(128)(4,1)S(1)}, s32[8]{0:T(128)S(1)}, pred[8]{0:T(512)(128)(4,1)}, s32[8]{0:T(128)S(1)}) fusion(s32[1,128]{1,0:T(1,128)} %param.7, s32[]{:T(128)S(6)} %select_n.51, s32[]{:T(128)S(6)} %select_n.57), kind=kLoop, calls=%fused_computation.147 | loop fusion | flops 96 | bytes 152 | tf_op jit(solution)/shard_map/jit(_take)/and | solution.py:90
  8.7 2.1 %gather_fusion.1 = bf16[8,128,768]{2,1,0:T(8,128)(2,1)S(1)} fusion(bf16[8,128,768]{2,1,0:T(8,128)(2,1)} %bitcast.76, s32[1024]{0:T(1024)S(1)} %pad_clamp_fusion.2), kind=kCustom, calls=%fused_computation.clone | custom fusion | bytes 3145760 | tf_op jit(solution)/shard_map/jit(_take)/gather | solution.py:90
  10.8 1.7 %multiply_reduce_fusion.4 = (f32[8,128]{1,0:T(8,128)S(1)}, bf16[8,128,768]{2,1,0:T(8,128)(2,1)}) fusion(bf16[8,128,768]{2,1,0:T(8,128)(2,1)S(1)} %gather_fusion.1, pred[8]{0:T(512)(128)(4,1)S(1)} %get-tuple-element.76), kind=kLoop, calls=%fused_computation.7 | loop fusion | flops 3144704 | bytes 3149832 | tf_op jit(solution)/shard_map/reduce_sum | solution.py:13
  13.1 1.3 %collective-permute-start.1 = (bf16[1024,768]{1,0:T(8,128)(2,1)}, bf16[1024,768]{1,0:T(8,128)(2,1)S(1)}, u32[]{:S(2)}, u32[]{:S(2)}) collective-permute-start(bf16[1024,768]{1,0:T(8,128)(2,1)} %bitcast.4), channel_id=1, source_target_pairs={{2,0},{4,2},{6,4},{14,6},{12,14},{10,12},{8,10},{1,8},{3,1},{5,3},... | collective-permute-start | bytes 4718600 | tf_op jit(solution)/shard_map/ppermute | solution.py:97
  15.2 1.8 %fusion.27 = f32[128]{0:T(128)} fusion(bf16[8,128,768]{2,1,0:T(8,128)(2,1)} %get-tuple-element.73, f32[128]{0:T(128)S(1)} %get-tuple-element.93), kind=kOutput, calls=%fused_computation.62 | convolution fusion | flops 25247616 | bytes 198144 | tf_op jit(solution)/shard_map/dot_general | solution.py:73
  18.1 1.2 slice.394
  19.3 2.1 %fusion.26 = f32[128]{0:T(128)} fusion(bf16[8,128,768]{2,1,0:T(8,128)(2,1)} %get-tuple-element.73, f32[128]{0:T(128)S(1)} %get-tuple-element.94), kind=kOutput, calls=%fused_computation.61 | convolution fusion | flops 25247616 | bytes 198144 | tf_op jit(solution)/shard_map/dot_general | solution.py:73
  23.6 1.3 %fusion.6 = f32[512]{0:T(512)} fusion(bf16[512,768]{1,0:T(8,128)(2,1)S(1)} %bitcast.81, f32[512]{0:T(512)S(1)} %slice_bitcast_fusion.15), kind=kOutput, calls=%fused_computation.23 | convolution fusion | flops 403963392 | bytes 790528 | tf_op jit(solution)/shard_map/dot_general | solution.py:73
  25.9 23.8 %collective-permute-done.1 = bf16[1024,768]{1,0:T(8,128)(2,1)S(1)} collective-permute-done((bf16[1024,768]{1,0:T(8,128)(2,1)}, bf16[1024,768]{1,0:T(8,128)(2,1)S(1)}, u32[]{:S(2)}, u32[]{:S(2)}) %collective-permute-start.1) | collective-permute-done | bytes 1572896 | tf_op jit(solution)/shard_map/ppermute | solution.py:97
  50.7 3.3 %gather_fusion.2 = bf16[8,128,768]{2,1,0:T(8,128)(2,1)} fusion(bf16[8,128,768]{2,1,0:T(8,128)(2,1)} %bitcast.8, s32[1024]{0:T(1024)} %pad_clamp_fusion.1), kind=kCustom, calls=%fused_computation.1.clone | custom fusion | bytes 3145760 | tf_op jit(solution)/shard_map/jit(_take)/gather | solution.py:119
  54.0 2.0 %multiply_reduce_fusion.1 = (f32[8,128]{1,0:T(8,128)S(1)}, bf16[8,128,768]{2,1,0:T(8,128)(2,1)S(1)}) fusion(bf16[8,128,768]{2,1,0:T(8,128)(2,1)} %gather_fusion.2, pred[8]{0:T(512)(128)(4,1)} %get-tuple-element.124), kind=kLoop, calls=%fused_computation.4 | loop fusion | flops 3144704 | bytes 3149832 | tf_op jit(solution)/shard_map/reduce_sum | solution.py:13
  56.2 16.3 %collective-permute-done.4 = bf16[1024,768]{1,0:T(8,128)(2,1)} collective-permute-done((bf16[1024,768]{1,0:T(8,128)(2,1)}, bf16[1024,768]{1,0:T(8,128)(2,1)}, u32[]{:S(2)}, u32[]{:S(2)}) %collective-permute-start.4) | collective-permute-done | bytes 1572896 | tf_op jit(solution)/shard_map/ppermute | solution.py:97
  72.6 1.8 %multiply_reduce_fusion = f32[1024]{0:T(1024)S(1)} fusion(bf16[1024,768]{1,0:T(8,128)(2,1)} %collective-permute-done.4), kind=kLoop, calls=%fused_computation.3 | loop fusion | flops 2358272 | bytes 1576960 | tf_op jit(solution)/shard_map/reduce_sum | solution.py:13
  74.5 1.3 %fusion.93 = (f32[256]{0:T(256)S(1)}, f32[128]{0:T(128)S(1)}) fusion(bf16[128,768]{1,0:T(8,128)(2,1)S(1)} %get-tuple-element.85, bf16[128,768]{1,0:T(8,128)(2,1)S(1)} %get-tuple-element.83, bf16[8,128,768]{2,1,0:T(8,128)(2,1)} %get-tuple-element.73, f32[256]{0:T(256)S(1)} %get-tuple-element.126, f32[128]{0:T(128)S(1)} %copy-done.16), kind=kOutput, calls=%fused_computation.208 | convolution fusion | flops 51314304 | bytes 592896 | tf_op jit(solution)/shard_map/dot_general | solution.py:73
  75.8 1.3 %fusion.94 = (f32[256]{0:T(256)S(1)}, f32[128]{0:T(128)S(1)}) fusion(bf16[128,768]{1,0:T(8,128)(2,1)S(1)} %get-tuple-element.84, bf16[128,768]{1,0:T(8,128)(2,1)S(1)} %get-tuple-element.82, bf16[8,128,768]{2,1,0:T(8,128)(2,1)} %get-tuple-element.73, f32[256]{0:T(256)S(1)} %get-tuple-element.123, f32[128]{0:T(128)S(1)} %copy-done.13), kind=kOutput, calls=%fused_computation.209 | convolution fusion | flops 51314304 | bytes 592896 | tf_op jit(solution)/shard_map/dot_general | solution.py:73
  77.2 1.2 exponential_reduce_fusion.2
  80.8 1.3 %fusion.90 = (f32[1024]{0:T(1024)S(1)}, f32[512]{0:T(512)S(1)}) fusion(bf16[512,768]{1,0:T(8,128)(2,1)S(1)} %bitcast.82, bf16[512,768]{1,0:T(8,128)(2,1)S(1)} %bitcast.77, bf16[512,768]{1,0:T(8,128)(2,1)S(1)} %slice.396, f32[1024]{0:T(1024)S(1)} %get-tuple-element.107, f32[512]{0:T(512)S(1)} %copy-done.7), kind=kOutput, calls=%fused_computation.205 | convolution fusion | flops 811596288 | bytes 2371584 | tf_op jit(solution)/shard_map/dot_general | solution.py:73
  86.8 1.3 %fusion.89 = (f32[1024]{0:T(1024)S(1)}, f32[512]{0:T(512)S(1)}) fusion(bf16[512,768]{1,0:T(8,128)(2,1)S(1)} %slice.395, bf16[512,768]{1,0:T(8,128)(2,1)S(1)} %bitcast.79, bf16[1024,768]{1,0:T(8,128)(2,1)S(1)} %collective-permute-done.1, f32[1024]{0:T(1024)S(1)} %get-tuple-element.106, f32[512]{0:T(512)S(1)} %slice.317), kind=kOutput, calls=%fused_computation.204 | convolution fusion | flops 811596288 | bytes 2371584 | tf_op jit(solution)/shard_map/dot_general | solution.py:73
  89.3 2.4 %fusion.88 = (f32[1024]{0:T(1024)S(1)}, f32[512]{0:T(512)S(1)}) fusion(bf16[512,768]{1,0:T(8,128)(2,1)S(1)} %bitcast.80, bf16[512,768]{1,0:T(8,128)(2,1)S(1)} %slice.396, bf16[1024,768]{1,0:T(8,128)(2,1)} %collective-permute-done.4, f32[1024]{0:T(1024)S(1)} %get-tuple-element.107, f32[512]{0:T(512)S(1)} %slice-done), kind=kOutput, calls=%fused_computation.203 | convolution fusion | flops 811596288 | bytes 2371584 | tf_op jit(solution)/shard_map/dot_general | solution.py:73
  91.7 1.5 %fusion.91 = (f32[512]{0:T(512)S(1)}, f32[256]{0:T(256)S(1)}) fusion(bf16[256,768]{1,0:T(8,128)(2,1)S(1)} %bitcast.87, bf16[256,768]{1,0:T(8,128)(2,1)S(1)} %slice.400, bf16[1024,768]{1,0:T(8,128)(2,1)} %collective-permute-done.4, f32[512]{0:T(512)S(1)} %get-tuple-element.119, f32[256]{0:T(256)S(1)} %slice.375), kind=kOutput, calls=%fused_computation.206 | convolution fusion | flops 203685120 | bytes 1185792 | tf_op jit(solution)/shard_map/dot_general | solution.py:73
  93.3 1.3 %fusion.52 = (f32[256]{0:T(256)S(1)}, f32[128]{0:T(128)S(1)}) fusion(f32[128]{0:T(128)S(1)} %get-tuple-element.99, f32[256]{0:T(256)S(1)} %get-tuple-element.123, bf16[128,768]{1,0:T(8,128)(2,1)S(1)} %get-tuple-element.84, bf16[128,768]{1,0:T(8,128)(2,1)S(1)} %get-tuple-element.82, bf16[1024,768]{1,0:T(8,128)(2,1)} %collective-permute-done.4), kind=kOutput, calls=%fused_computation.104 | convolution fusion | flops 51314304 | bytes 592896 | tf_op jit(solution)/shard_map/dot_general | solution.py:73
  94.7 1.3 %fusion.54 = (f32[256]{0:T(256)S(1)}, f32[128]{0:T(128)S(1)}) fusion(f32[128]{0:T(128)S(1)} %get-tuple-element.100, f32[256]{0:T(256)S(1)} %get-tuple-element.126, bf16[128,768]{1,0:T(8,128)(2,1)S(1)} %get-tuple-element.85, bf16[128,768]{1,0:T(8,128)(2,1)S(1)} %get-tuple-element.83, bf16[1024,768]{1,0:T(8,128)(2,1)} %collective-permute-done.4), kind=kOutput, calls=%fused_computation.106 | convolution fusion | flops 51314304 | bytes 592896 | tf_op jit(solution)/shard_map/dot_general | solution.py:73
  96.0 1.7 %collective-permute-start.5 = (f32[1024]{0:T(1024)S(1)}, f32[1024]{0:T(1024)S(1)}, u32[]{:S(2)}, u32[]{:S(2)}) collective-permute-start(f32[1024]{0:T(1024)S(1)} %pad_maximum_fusion.17), channel_id=1, source_target_pairs={{0,2},{2,4},{4,6},{6,14},{14,12},{12,10},{10,8},{8,1},{1,3},{3,5},... | collective-permute-start | bytes 12296 | tf_op jit(solution)/shard_map/ppermute | solution.py:104
  97.7 3.1 %collective-permute-start.6 = (f32[1024]{0:T(1024)S(1)}, f32[1024]{0:T(1024)S(1)}, u32[]{:S(2)}, u32[]{:S(2)}) collective-permute-start(f32[1024]{0:T(1024)S(1)} %pad_maximum_fusion.18), channel_id=1, source_target_pairs={{0,12},{2,10},{4,8},{6,1},{14,3},{12,5},{10,7},{8,15},{1,13},{3,11... | collective-permute-start | bytes 12296 | tf_op jit(solution)/shard_map/ppermute | solution.py:104
  100.9 1.3 %collective-permute-done.6 = f32[1024]{0:T(1024)S(1)} collective-permute-done((f32[1024]{0:T(1024)S(1)}, f32[1024]{0:T(1024)S(1)}, u32[]{:S(2)}, u32[]{:S(2)}) %collective-permute-start.6) | collective-permute-done | bytes 4128 | tf_op jit(solution)/shard_map/ppermute | solution.py:104
  102.2 2.3 %collective-permute-done.7 = f32[1024]{0:T(1024)S(1)} collective-permute-done((f32[1024]{0:T(1024)S(1)}, f32[1024]{0:T(1024)S(1)}, u32[]{:S(2)}, u32[]{:S(2)}) %collective-permute-start.7) | collective-permute-done | bytes 4128 | tf_op jit(solution)/shard_map/ppermute | solution.py:104
  105.1 1.3 %broadcast_in_dim.30 = f32[128,1,1]{2,1,0:T(1,128)} broadcast(f32[]{:T(128)} %get-tuple-element.70), dimensions={} | broadcast | bytes 516 | tf_op jit(solution)/shard_map/broadcast_in_dim | solution.py:68
  106.4 8.2 %all-to-all-start = ((f32[128,1,1]{2,1,0:T(1,128)}), f32[128,1,1]{2,1,0:T(1,128)S(1)}, u32[]{:S(2)}, u32[]{:S(2)}) async-start(f32[128,1,1]{2,1,0:T(1,128)} %broadcast_in_dim.30), calls=%async_computation | async-start | bytes 131072 | tf_op jit(solution)/shard_map/all_to_all | solution.py:68
  115.2 9.0 %all-to-all-done = f32[128,1,1]{2,1,0:T(1,128)S(1)} async-done(((f32[128,1,1]{2,1,0:T(1,128)}), f32[128,1,1]{2,1,0:T(1,128)S(1)}, u32[]{:S(2)}, u32[]{:S(2)}) %all-to-all-start) | async-done | bytes 544 | tf_op jit(solution)/shard_map/all_to_all | solution.py:68
  (116 shorter events, 17.6 us)
Async XLA Ops:
  0.0 50.7 %collective-permute-start.2 = (bf16[1024,768]{1,0:T(8,128)(2,1)}, bf16[1024,768]{1,0:T(8,128)(2,1)}, u32[]{:S(2)}, u32[]{:S(2)}) collective-permute-start(bf16[1024,768]{1,0:T(8,128)(2,1)} %param.6), channel_id=1, source_target_pairs={{12,0},{10,2},{8,4},{1,6},{3,14},{5,12},{7,10},{15,8},{13,1},{11,3... | collective-permute-start | bytes 4718600 | tf_op jit(solution)/shard_map/ppermute | solution.py:97
  12.4 12.4 %collective-permute-start = (bf16[1024,768]{1,0:T(8,128)(2,1)}, bf16[1024,768]{1,0:T(8,128)(2,1)S(1)}, u32[]{:S(2)}, u32[]{:S(2)}) collective-permute-start(bf16[1024,768]{1,0:T(8,128)(2,1)} %bitcast.4), channel_id=1, source_target_pairs={{1,0},{3,2},{5,4},{7,6},{15,14},{13,12},{11,10},{9,8},{0,1},{2,3},... | collective-permute-start | bytes 4718600 | tf_op jit(solution)/shard_map/ppermute | solution.py:97
  13.1 36.6 %collective-permute-start.1 = (bf16[1024,768]{1,0:T(8,128)(2,1)}, bf16[1024,768]{1,0:T(8,128)(2,1)S(1)}, u32[]{:S(2)}, u32[]{:S(2)}) collective-permute-start(bf16[1024,768]{1,0:T(8,128)(2,1)} %bitcast.4), channel_id=1, source_target_pairs={{2,0},{4,2},{6,4},{14,6},{12,14},{10,12},{8,10},{1,8},{3,1},{5,3},... | collective-permute-start | bytes 4718600 | tf_op jit(solution)/shard_map/ppermute | solution.py:97
  14.4 58.1 %collective-permute-start.4 = (bf16[1024,768]{1,0:T(8,128)(2,1)}, bf16[1024,768]{1,0:T(8,128)(2,1)}, u32[]{:S(2)}, u32[]{:S(2)}) collective-permute-start(bf16[1024,768]{1,0:T(8,128)(2,1)} %bitcast.4), channel_id=1, source_target_pairs={{9,0},{0,2},{2,4},{4,6},{6,14},{14,12},{12,10},{10,8},{8,1},{1,3},... | collective-permute-start | bytes 4718600 | tf_op jit(solution)/shard_map/ppermute | solution.py:97
  15.2 1.8 %copy-start.15 = (f32[128]{0:T(128)}, f32[128]{0:T(128)S(1)}, u32[]{:S(2)}) copy-start(f32[128]{0:T(128)S(1)} %get-tuple-element.93) | copy-start | bytes 1540
  15.2 6.3 %copy-start.12 = (f32[128]{0:T(128)}, f32[128]{0:T(128)S(1)}, u32[]{:S(2)}) copy-start(f32[128]{0:T(128)S(1)} %get-tuple-element.94) | copy-start | bytes 1540
  17.1 5.9 %copy-start.18 = (s32[8]{0:T(128)}, s32[8]{0:T(128)S(1)}, u32[]{:S(2)}) copy-start(s32[8]{0:T(128)S(1)} %select_reduce_fusion) | copy-start | bytes 100
  19.3 5.6 %copy-start = (bf16[4,128,768]{2,1,0:T(8,128)(2,1)}, bf16[4,128,768]{2,1,0:T(8,128)(2,1)S(1)}, u32[]{:S(2)}) copy-start(bf16[4,128,768]{2,1,0:T(8,128)(2,1)S(1)} %slice.394) | copy-start | bytes 2359300
  22.0 1.5 %copy-start.9 = (f32[256]{0:T(256)}, f32[256]{0:T(256)S(1)}, u32[]{:S(2)}) copy-start(f32[256]{0:T(256)S(1)} %slice_bitcast_fusion.17) | copy-start | bytes 3076
  23.6 1.3 %copy-start.6 = (f32[512]{0:T(512)}, f32[512]{0:T(512)S(1)}, u32[]{:S(2)}) copy-start(f32[512]{0:T(512)S(1)} %slice_bitcast_fusion.15) | copy-start | bytes 6148
  56.2 18.3 %copy-start.16 = (f32[128]{0:T(128)S(1)}, f32[128]{0:T(128)}, u32[]{:S(2)}) copy-start(f32[128]{0:T(128)} %copy-done.15) | copy-start | bytes 1540
  56.2 19.6 %copy-start.13 = (f32[128]{0:T(128)S(1)}, f32[128]{0:T(128)}, u32[]{:S(2)}) copy-start(f32[128]{0:T(128)} %copy-done.12) | copy-start | bytes 1540
  74.3 2.8 %copy-start.2 = (f32[1024]{0:T(1024)}, f32[1024]{0:T(1024)S(1)}, u32[]{:S(2)}) copy-start(f32[1024]{0:T(1024)S(1)} %multiply_reduce_fusion) | copy-start | bytes 12292
  74.4 3.9 %copy-start.17 = (f32[128]{0:T(128)S(1)}, f32[128]{0:T(128)}, u32[]{:S(2)}) copy-start(f32[128]{0:T(128)} %fusion.27) | copy-start | bytes 1540
  74.5 5.1 %copy-start.14 = (f32[128]{0:T(128)S(1)}, f32[128]{0:T(128)}, u32[]{:S(2)}) copy-start(f32[128]{0:T(128)} %fusion.26) | copy-start | bytes 1540
  74.5 5.1 %copy-start.3 = (f32[256]{0:T(256)S(1)}, f32[256]{0:T(256)}, u32[]{:S(2)}) copy-start(f32[256]{0:T(256)} %slice.326) | copy-start | bytes 3076
  74.5 5.1 %copy-start.4 = (f32[256]{0:T(256)S(1)}, f32[256]{0:T(256)}, u32[]{:S(2)}) copy-start(f32[256]{0:T(256)} %slice.328) | copy-start | bytes 3076
  75.8 3.8 %copy-start.10 = (f32[256]{0:T(256)S(1)}, f32[256]{0:T(256)}, u32[]{:S(2)}) copy-start(f32[256]{0:T(256)} %copy-done.9) | copy-start | bytes 3076
  79.6 1.1 copy-start.1
  79.7 1.1 copy-start.7
  84.5 0.7 copy-start.8
  86.8 1.3 %copy-start.5 = (f32[512]{0:T(512)S(1)}, f32[512]{0:T(512)}, u32[]{:S(2)}) copy-start(f32[512]{0:T(512)} %fusion.6) | copy-start | bytes 6148
  86.8 2.5 %slice-start = ((f32[1024]{0:T(1024)}), f32[512]{0:T(512)S(1)}, s32[]{:S(2)}) async-start(f32[1024]{0:T(1024)} %copy-done.2), calls=%async_computation.1 | async-start | bytes 4096 | tf_op jit(solution)/shard_map/slice | solution.py:149
  88.1 12.7 %collective-permute-start.3 = (f32[1024]{0:T(1024)S(1)}, f32[1024]{0:T(1024)S(1)}, u32[]{:S(2)}, u32[]{:S(2)}) collective-permute-start(f32[1024]{0:T(1024)S(1)} %pad_maximum_fusion.16), channel_id=1, source_target_pairs={{0,1},{2,3},{4,5},{6,7},{14,15},{12,13},{10,11},{8,9},{1,0},{3,2},... | collective-permute-start | bytes 12296 | tf_op jit(solution)/shard_map/ppermute | solution.py:104
  93.3 7.6 %copy-start.19 = (s32[8]{0:T(128)S(1)}, s32[8]{0:T(128)}, u32[]{:S(2)}) copy-start(s32[8]{0:T(128)} %copy-done.18) | copy-start | bytes 100
  93.3 21.3 %copy-start.11 = (s32[8]{0:T(128)S(1)}, s32[8]{0:T(128)}, u32[]{:S(2)}) copy-start(s32[8]{0:T(128)} %fusion.63) | copy-start | bytes 100
  96.0 4.9 %collective-permute-start.5 = (f32[1024]{0:T(1024)S(1)}, f32[1024]{0:T(1024)S(1)}, u32[]{:S(2)}, u32[]{:S(2)}) collective-permute-start(f32[1024]{0:T(1024)S(1)} %pad_maximum_fusion.17), channel_id=1, source_target_pairs={{0,2},{2,4},{4,6},{6,14},{14,12},{12,10},{10,8},{8,1},{1,3},{3,5},... | collective-permute-start | bytes 12296 | tf_op jit(solution)/shard_map/ppermute | solution.py:104
  97.7 4.4 %collective-permute-start.6 = (f32[1024]{0:T(1024)S(1)}, f32[1024]{0:T(1024)S(1)}, u32[]{:S(2)}, u32[]{:S(2)}) collective-permute-start(f32[1024]{0:T(1024)S(1)} %pad_maximum_fusion.18), channel_id=1, source_target_pairs={{0,12},{2,10},{4,8},{6,1},{14,3},{12,5},{10,7},{8,15},{1,13},{3,11... | collective-permute-start | bytes 12296 | tf_op jit(solution)/shard_map/ppermute | solution.py:104
  100.8 3.6 %collective-permute-start.7 = (f32[1024]{0:T(1024)S(1)}, f32[1024]{0:T(1024)S(1)}, u32[]{:S(2)}, u32[]{:S(2)}) collective-permute-start(f32[1024]{0:T(1024)S(1)} %pad_maximum_fusion.19), channel_id=1, source_target_pairs={{0,9},{2,0},{4,2},{6,4},{14,6},{12,14},{10,12},{8,10},{1,8},{3,1},... | collective-permute-start | bytes 12296 | tf_op jit(solution)/shard_map/ppermute | solution.py:104
  106.4 17.8 %all-to-all-start = ((f32[128,1,1]{2,1,0:T(1,128)}), f32[128,1,1]{2,1,0:T(1,128)S(1)}, u32[]{:S(2)}, u32[]{:S(2)}) async-start(f32[128,1,1]{2,1,0:T(1,128)} %broadcast_in_dim.30), calls=%async_computation | async-start | bytes 131072 | tf_op jit(solution)/shard_map/all_to_all | solution.py:68

commit v5 on v3

--- a/solution.py
+++ b/solution.py
@@ -87,7 +87,10 @@
     per_device = row_count // BLK
     order = lax.dynamic_slice_in_dim(block_order[0], position * per_device, per_device)
     blocks = embeddings.reshape(per_device, BLK, width)
-    ordered = jnp.take(blocks, order, axis=0).reshape(row_count, width)
+    pick = (order[:, None] == jnp.arange(per_device, dtype=jnp.int32)[None, :]).astype(embeddings.dtype)
+    ordered = jnp.einsum(
+        "sl,lrd->srd", pick, blocks, preferred_element_type=jnp.float32
+    ).astype(embeddings.dtype).reshape(row_count, width)
     spans = [(start * BLK, end * BLK) for start, end in class_spans(per_device)]
 
     ring = member_ring(member_count)
@@ -108,17 +111,24 @@
         )
 
     late = offsets[-1]
+    cut = spans[0][1]
     held = {0: ordered}
     for offset in offsets[1:]:
-        held[offset] = fetch(ordered, offset)
-    norms = {}
+        if offset == late:
+            head = fetch(ordered[:cut], offset)
+            tail = fetch(ordered[cut:], offset)
+            held[offset] = jnp.concatenate([head, tail])
+            late_norms = jnp.concatenate([squared(head), squared(tail)])
+        else:
+            held[offset] = fetch(ordered, offset)
+    norms = {late: late_norms}
     partial = {offset: [None] * len(spans) for offset in offsets}
 
     def add(offset, index, value):
         slot = partial[offset]
         slot[index] = value if slot[index] is None else slot[index] + value
 
-    def blocks(chosen):
+    def blocks(chosen, classes=None):
         for offset in {o for a, b, _ in chosen for o in (a, b)} | {0}:
             if offset not in norms:
                 norms[offset] = squared(held[offset])
@@ -126,6 +136,8 @@
         for a, b, both in chosen:
             groups.setdefault((a, both), []).append(b)
         for index, (start, end) in enumerate(spans):
+            if classes is not None and index not in classes:
+                continue
             for (a, both), others in groups.items():
                 if not both:
                     for b in others:
@@ -148,8 +160,9 @@
 
     late_pairs = [p for p in pairs if late in p[:2]]
     blocks([(0, 0, False)] + [p for p in pairs if late not in p[:2]])
+    blocks(late_pairs, {0})
     partial = lax.optimization_barrier(partial)
-    blocks(late_pairs)
+    blocks(late_pairs, set(range(1, len(spans))))
 
     def joined(offset):
         parts = [
@@ -172,7 +185,7 @@
     back = jnp.sum(
         jnp.where(order[None, :] == spots[:, None], spots[None, :], 0), axis=1
     )
-    stored = jnp.take(inverse, back, axis=0).reshape(-1)
+    stored = inverse.at[back].get(mode="promise_in_bounds").reshape(-1)
     return stored * (everything / total)
 
 

time: 120 us -> 156 us (1.30)
  matrix products: 13.1 us -> 35.9 us
  local copies, waits for them, and re-layouts: 3.05 us -> 19.6 us
  waiting for transfers between devices: 75.2 us -> 65.8 us
  other arithmetic: 6.27 us -> 10.3 us
    dot_general x24, matrix products: 13.1 us -> 34.8 us  [kernel_sums(): lax.dot_general(left, right, (((1,), (1,)), ((), ())), preferred_element_...]
    slice x9, local copies, waits for them, and re-layouts: 0.32 us -> 9.83 us  [blocks(): held[b][start:end]]
    ppermute x4 -> x5, waiting for transfers between devices: 63.4 us -> 53.9 us  [fetch(): lax.ppermute(value, 'mem', [(ring[(r + offset) % member_count], ring[r])...]
    reduce_sum x5, other arithmetic: 2.09 us -> 8.07 us  [squared(): return jnp.sum(jnp.square(values.astype(jnp.float32)), axis=1)]
    slice x2 -> x5, local copies, waits for them, and re-layouts: 0.08 us -> 3.61 us  [blocks(): held[a][start:end]]
    ppermute x4 -> x5, starting transfers between devices: 6.38 us -> 8.08 us  [fetch(): lax.ppermute(value, 'mem', [(ring[(r + offset) % member_count], ring[r])...]
  transfers between devices with their start and end apart: 9 -> 10, of which waited for: 6 -> 5; matrix products, arithmetic and copies ran while one was open for 6% -> 11% of each run, Pallas kernels for 0% -> 0%
where the time goes in v5:
time: 156 us; the launch traced here: 154 us
  waiting for transfers between devices  65.8 us (42%)
  matrix products  35.9 us (23%)
  starting transfers between devices  21.7 us (14%)
  local copies, waits for them, and re-layouts  19.6 us (13%)
  other arithmetic  10.3 us (7%)
    ppermute x5, waiting for transfers between devices, fetch(): lax.ppermute(value, 'mem', [(ring[(r + offset) % member_count], ring[r])...  53.9 us
    dot_general x24, matrix products, kernel_sums(): lax.dot_general(left, right, (((1,), (1,)), ((), ())), preferred_element_...  34.8 us
    all_to_all x1, starting transfers between devices, grand_total(): lax.all_to_all(jnp.broadcast_to(value, (size,)), axes, 0, 0, tiled=True)  9.9 us
    slice x9, local copies, waits for them, and re-layouts, blocks(): held[b][start:end]  9.83 us
    all_to_all x1, waiting for transfers between devices, grand_total(): lax.all_to_all(jnp.broadcast_to(value, (size,)), axes, 0, 0, tiled=True)  8.97 us
    ppermute x5, starting transfers between devices, fetch(): lax.ppermute(value, 'mem', [(ring[(r + offset) % member_count], ring[r])...  8.08 us
    reduce_sum x5, other arithmetic, squared(): return jnp.sum(jnp.square(values.astype(jnp.float32)), axis=1)  8.07 us
    ppermute x4, starting transfers between devices, give_back(): lax.ppermute(value, 'mem', [(ring[r], ring[(r + offset) % member_count])...  3.7 us
  transfers between devices with their start and end apart: 10, of which 5 were waited for; matrix products, arithmetic and copies ran while one was open for 11% of the time, Pallas kernels for 0%

profile of v5, /device:TPU:0, one launch (start us, length us, event | category | flops | bytes accessed | tf_op | source)
XLA Modules:
  0.0 154.4 jit_solution(18107086678998955139)
XLA Ops:
  2.6 1.5 copy.51
  4.0 4.3 %collective-permute-start.2 = (bf16[1024,768]{1,0:T(8,128)(2,1)}, bf16[1024,768]{1,0:T(8,128)(2,1)}, u32[]{:S(2)}, u32[]{:S(2)}) collective-permute-start(bf16[1024,768]{1,0:T(8,128)(2,1)} %bitcast.5), channel_id=1, source_target_pairs={{12,0},{10,2},{8,4},{1,6},{3,14},{5,12},{7,10},{15,8},{13,1},{11,3... | collective-permute-start | bytes 4718600 | tf_op jit(solution)/shard_map/ppermute | solution.py:100
  12.9 1.8 %collective-permute-start.3 = (bf16[512,768]{1,0:T(8,128)(2,1)}, bf16[512,768]{1,0:T(8,128)(2,1)}, u32[]{:S(2)}, u32[]{:S(2)}) collective-permute-start(bf16[512,768]{1,0:T(8,128)(2,1)} %bitcast.4), channel_id=1, source_target_pairs={{9,0},{0,2},{2,4},{4,6},{6,14},{14,12},{12,10},{10,8},{8,1},{1,3},... | collective-permute-start | bytes 2359304 | tf_op jit(solution)/shard_map/ppermute | solution.py:100
  14.7 1.6 %fusion.121 = (bf16[1,128,768]{2,0,1:T(2,128)(2,1)}, bf16[1,128,768]{2,0,1:T(2,128)(2,1)}) fusion(bf16[8,128,768]{2,0,1:T(8,128)(2,1)S(1)} %get-tuple-element.120), kind=kLoop, calls=%fused_computation.209 | loop fusion | bytes 786432 | tf_op jit(solution)/shard_map/slice | solution.py:145
  16.5 1.4 fusion.27
  17.9 1.4 fusion.28
  19.3 2.2 %fusion.7 = f32[512]{0:T(512)S(1)} fusion(bf16[512,768]{1,0:T(8,128)(2,1)} %bitcast.4, f32[512]{0:T(512)S(1)} %bitcast.59), kind=kOutput, calls=%fused_computation.22 | convolution fusion | flops 403963392 | bytes 790528 | tf_op jit(solution)/shard_map/dot_general | solution.py:73
  22.6 38.4 %collective-permute-done.5 = bf16[512,768]{1,0:T(8,128)(2,1)} collective-permute-done((bf16[512,768]{1,0:T(8,128)(2,1)}, bf16[512,768]{1,0:T(8,128)(2,1)}, u32[]{:S(2)}, u32[]{:S(2)}) %collective-permute-start.5) | collective-permute-done | bytes 786464 | tf_op jit(solution)/shard_map/ppermute | solution.py:100
  61.0 1.4 multiply_reduce_fusion.4
  62.4 15.5 %collective-permute-done.3 = bf16[512,768]{1,0:T(8,128)(2,1)} collective-permute-done((bf16[512,768]{1,0:T(8,128)(2,1)}, bf16[512,768]{1,0:T(8,128)(2,1)}, u32[]{:S(2)}, u32[]{:S(2)}) %collective-permute-start.3) | collective-permute-done | bytes 786464 | tf_op jit(solution)/shard_map/ppermute | solution.py:100
  77.9 1.4 multiply_reduce_fusion.5
  79.2 1.8 %multiply_reduce_fusion.2 = f32[1024]{0:T(1024)S(1)} fusion(bf16[1024,768]{1,0:T(8,128)(2,1)} %collective-permute-done), kind=kLoop, calls=%fused_computation.3 | loop fusion | flops 2358272 | bytes 1576960 | tf_op jit(solution)/shard_map/reduce_sum | solution.py:13
  81.0 1.8 %multiply_reduce_fusion = f32[1024]{0:T(1024)S(1)} fusion(bf16[1024,768]{1,0:T(8,128)(2,1)} %collective-permute-done.2), kind=kLoop, calls=%fused_computation.1 | loop fusion | flops 2358272 | bytes 1576960 | tf_op jit(solution)/shard_map/reduce_sum | solution.py:13
  82.9 1.8 %multiply_reduce_fusion.1 = f32[1024]{0:T(1024)S(1)} fusion(bf16[1024,768]{1,0:T(8,128)(2,1)} %collective-permute-done.1), kind=kLoop, calls=%fused_computation.2 | loop fusion | flops 2358272 | bytes 1576960 | tf_op jit(solution)/shard_map/reduce_sum | solution.py:13
  87.1 2.4 %fusion.113 = (f32[1024]{0:T(1024)S(1)}, f32[512]{0:T(512)S(1)}) fusion(bf16[512,768]{1,0:T(8,128)(2,1)} %bitcast.4, bf16[512,768]{1,0:T(8,128)(2,1)S(1)} %slice.363, bf16[512,768]{1,0:T(8,128)(2,1)S(1)} %slice.362, f32[1024]{0:T(1024)S(1)} %get-tuple-element.100, f32[512]{0:T(512)S(1)} %bitcast.60), kind=kOutput, calls=%fused_computation.202 | convolution fusion | flops 811596288 | bytes 2371584 | tf_op jit(solution)/shard_map/dot_general | solution.py:73
  89.6 2.1 %exponential_reduce_fusion = f32[512]{0:T(512)S(1)} fusion(f32[512]{0:T(512)S(1)} %slice.292, bf16[512,768]{1,0:T(8,128)(2,1)} %bitcast.4, f32[512]{0:T(512)S(1)} %bitcast.61, bf16[1024,768]{1,0:T(8,128)(2,1)} %collective-permute-done), kind=kOutput, calls=%fused_computation.63 | convolution fusion | flops 403963392 | bytes 1579008 | tf_op jit(solution)/shard_map/dot_general | solution.py:73
  99.7 1.3 fusion.61
  103.4 1.3 fusion.63
  104.8 1.3 fusion.55
  107.3 2.2 %fusion.29 = (f32[512]{0:T(512)S(1)}, f32[512]{0:T(512)S(1)}) fusion(f32[512]{0:T(512)S(1)} %slice.295, f32[512]{0:T(512)S(1)} %slice.292, bf16[1024,768]{1,0:T(8,128)(2,1)} %collective-permute-done, bf16[1024,768]{1,0:T(8,128)(2,1)} %collective-permute-done.2), kind=kOutput, calls=%fused_computation.64 | convolution fusion | flops 404225024 | bytes 1581056 | tf_op jit(solution)/shard_map/dot_general | solution.py:73
  109.5 2.4 %fusion.111 = (f32[512]{0:T(512)S(1)}, f32[1024]{0:T(1024)S(1)}) fusion(bf16[512,768]{1,0:T(8,128)(2,1)} %collective-permute-done.3, bf16[512,768]{1,0:T(8,128)(2,1)S(1)} %slice.363, bf16[512,768]{1,0:T(8,128)(2,1)S(1)} %slice.362, f32[1024]{0:T(1024)S(1)} %get-tuple-element.100, f32[512]{0:T(512)S(1)} %multiply_reduce_fusion.5), kind=kOutput, calls=%fused_computation.200 | convolution fusion | flops 811596288 | bytes 2371584 | tf_op jit(solution)/shard_map/dot_general | solution.py:73
  111.9 2.4 %fusion.112 = (f32[1024]{0:T(1024)S(1)}, f32[512]{0:T(512)S(1)}) fusion(bf16[512,768]{1,0:T(8,128)(2,1)S(1)} %slice.361, bf16[512,768]{1,0:T(8,128)(2,1)S(1)} %slice.363, bf16[1024,768]{1,0:T(8,128)(2,1)} %collective-permute-done.1, f32[1024]{0:T(1024)S(1)} %get-tuple-element.99, f32[512]{0:T(512)S(1)} %slice.294), kind=kOutput, calls=%fused_computation.201 | convolution fusion | flops 811596288 | bytes 2371584 | tf_op jit(solution)/shard_map/dot_general | solution.py:73
  114.4 1.5 fusion.43
  117.0 1.4 exponential_reduce_fusion.1
  118.3 1.6 %fusion.34 = (f32[512]{0:T(512)S(1)}, f32[256]{0:T(256)S(1)}) fusion(f32[512]{0:T(512)S(1)} %get-tuple-element.113, f32[256]{0:T(256)S(1)} %slice.303, bf16[256,768]{1,0:T(8,128)(2,1)S(1)} %slice.366, bf16[256,768]{1,0:T(8,128)(2,1)S(1)} %slice.368, bf16[1024,768]{1,0:T(8,128)(2,1)} %collective-permute-done.1), kind=kOutput, calls=%fused_computation.72 | convolution fusion | flops 203685120 | bytes 1185792 | tf_op jit(solution)/shard_map/dot_general | solution.py:73
  121.2 1.3 fusion.58
  122.6 1.7 %fusion.114 = (f32[512]{0:T(512)S(1)}, f32[256]{0:T(256)S(1)}) fusion(bf16[256,768]{1,0:T(8,128)(2,1)S(1)} %slice.368, bf16[256,768]{1,0:T(8,128)(2,1)S(1)} %slice.367, bf16[512,768]{1,0:T(8,128)(2,1)} %collective-permute-done.5, f32[512]{0:T(512)S(1)} %get-tuple-element.114, f32[256]{0:T(256)S(1)} %slice-done), kind=kOutput, calls=%fused_computation.203 | convolution fusion | flops 203685120 | bytes 1185792 | tf_op jit(solution)/shard_map/dot_general | solution.py:73
  124.3 2.0 %collective-permute-start.8 = (f32[1024]{0:T(1024)S(1)}, f32[1024]{0:T(1024)S(1)}, u32[]{:S(2)}, u32[]{:S(2)}) collective-permute-start(f32[1024]{0:T(1024)S(1)} %pad_maximum_fusion.19), channel_id=1, source_target_pairs={{0,9},{2,0},{4,2},{6,4},{14,6},{12,14},{10,12},{8,10},{1,8},{3,1},... | collective-permute-start | bytes 12296 | tf_op jit(solution)/shard_map/ppermute | solution.py:107
  126.3 1.6 %collective-permute-start.7 = (f32[1024]{0:T(1024)S(1)}, f32[1024]{0:T(1024)S(1)}, u32[]{:S(2)}, u32[]{:S(2)}) collective-permute-start(f32[1024]{0:T(1024)S(1)} %pad_maximum_fusion.18), channel_id=1, source_target_pairs={{0,12},{2,10},{4,8},{6,1},{14,3},{12,5},{10,7},{8,15},{1,13},{3,11... | collective-permute-start | bytes 12296 | tf_op jit(solution)/shard_map/ppermute | solution.py:107
  128.1 2.5 %collective-permute-done.7 = f32[1024]{0:T(1024)S(1)} collective-permute-done((f32[1024]{0:T(1024)S(1)}, f32[1024]{0:T(1024)S(1)}, u32[]{:S(2)}, u32[]{:S(2)}) %collective-permute-start.7) | collective-permute-done | bytes 4128 | tf_op jit(solution)/shard_map/ppermute | solution.py:107
  132.9 9.9 %all-to-all-start = ((f32[128,1,1]{2,1,0:T(1,128)}), f32[128,1,1]{2,1,0:T(1,128)S(1)}, u32[]{:S(2)}, u32[]{:S(2)}) async-start(f32[128,1,1]{2,1,0:T(1,128)} %broadcast_in_dim.9), calls=%async_computation | async-start | bytes 131072 | tf_op jit(solution)/shard_map/all_to_all | solution.py:68
  143.4 9.0 %all-to-all-done = f32[128,1,1]{2,1,0:T(1,128)S(1)} async-done(((f32[128,1,1]{2,1,0:T(1,128)}), f32[128,1,1]{2,1,0:T(1,128)S(1)}, u32[]{:S(2)}, u32[]{:S(2)}) %all-to-all-start) | async-done | bytes 544 | tf_op jit(solution)/shard_map/all_to_all | solution.py:68
  (84 shorter events, 29.1 us)
Async XLA Ops:
  0.0 1.4 copy-start
  4.0 75.2 %collective-permute-start = (bf16[1024,768]{1,0:T(8,128)(2,1)}, bf16[1024,768]{1,0:T(8,128)(2,1)}, u32[]{:S(2)}, u32[]{:S(2)}) collective-permute-start(bf16[1024,768]{1,0:T(8,128)(2,1)} %bitcast.5), channel_id=1, source_target_pairs={{1,0},{3,2},{5,4},{7,6},{15,14},{13,12},{11,10},{9,8},{0,1},{2,3},... | collective-permute-start | bytes 4718600 | tf_op jit(solution)/shard_map/ppermute | solution.py:100
  4.0 77.0 %collective-permute-start.2 = (bf16[1024,768]{1,0:T(8,128)(2,1)}, bf16[1024,768]{1,0:T(8,128)(2,1)}, u32[]{:S(2)}, u32[]{:S(2)}) collective-permute-start(bf16[1024,768]{1,0:T(8,128)(2,1)} %bitcast.5), channel_id=1, source_target_pairs={{12,0},{10,2},{8,4},{1,6},{3,14},{5,12},{7,10},{15,8},{13,1},{11,3... | collective-permute-start | bytes 4718600 | tf_op jit(solution)/shard_map/ppermute | solution.py:100
  8.3 74.6 %collective-permute-start.1 = (bf16[1024,768]{1,0:T(8,128)(2,1)}, bf16[1024,768]{1,0:T(8,128)(2,1)}, u32[]{:S(2)}, u32[]{:S(2)}) collective-permute-start(bf16[1024,768]{1,0:T(8,128)(2,1)} %bitcast.5), channel_id=1, source_target_pairs={{2,0},{4,2},{6,4},{14,6},{12,14},{10,12},{8,10},{1,8},{3,1},{5,3},... | collective-permute-start | bytes 4718600 | tf_op jit(solution)/shard_map/ppermute | solution.py:100
  10.8 50.2 %collective-permute-start.5 = (bf16[512,768]{1,0:T(8,128)(2,1)}, bf16[512,768]{1,0:T(8,128)(2,1)}, u32[]{:S(2)}, u32[]{:S(2)}) collective-permute-start(bf16[512,768]{1,0:T(8,128)(2,1)} %bitcast.8), channel_id=1, source_target_pairs={{9,0},{0,2},{2,4},{4,6},{6,14},{14,12},{12,10},{10,8},{8,1},{1,3},... | collective-permute-start | bytes 2359304 | tf_op jit(solution)/shard_map/ppermute | solution.py:100
  12.9 65.0 %collective-permute-start.3 = (bf16[512,768]{1,0:T(8,128)(2,1)}, bf16[512,768]{1,0:T(8,128)(2,1)}, u32[]{:S(2)}, u32[]{:S(2)}) collective-permute-start(bf16[512,768]{1,0:T(8,128)(2,1)} %bitcast.4), channel_id=1, source_target_pairs={{9,0},{0,2},{2,4},{4,6},{6,14},{14,12},{12,10},{10,8},{8,1},{1,3},... | collective-permute-start | bytes 2359304 | tf_op jit(solution)/shard_map/ppermute | solution.py:100
  62.4 20.5 %copy-start.3 = (f32[512]{0:T(512)}, f32[512]{0:T(512)S(1)}, u32[]{:S(2)}) copy-start(f32[512]{0:T(512)S(1)} %multiply_reduce_fusion.4) | copy-start | bytes 6148
  93.7 2.7 %copy-start.2 = (bf16[1,128,768]{2,0,1:T(2,128)(2,1)S(1)}, bf16[1,128,768]{2,0,1:T(2,128)(2,1)}, u32[]{:S(2)}) copy-start(bf16[1,128,768]{2,0,1:T(2,128)(2,1)} %get-tuple-element.78) | copy-start | bytes 589828
  94.3 3.8 %copy-start.1 = (bf16[1,128,768]{2,0,1:T(2,128)(2,1)S(1)}, bf16[1,128,768]{2,0,1:T(2,128)(2,1)}, u32[]{:S(2)}) copy-start(bf16[1,128,768]{2,0,1:T(2,128)(2,1)} %get-tuple-element.77) | copy-start | bytes 589828
  119.9 2.7 %slice-start = ((f32[512]{0:T(512)}), f32[256]{0:T(256)S(1)}, s32[]{:S(2)}) async-start(f32[512]{0:T(512)} %copy-done.3), calls=%async_computation.1 | async-start | bytes 2048 | tf_op jit(solution)/shard_map/slice | solution.py:153
  124.3 3.8 %collective-permute-start.8 = (f32[1024]{0:T(1024)S(1)}, f32[1024]{0:T(1024)S(1)}, u32[]{:S(2)}, u32[]{:S(2)}) collective-permute-start(f32[1024]{0:T(1024)S(1)} %pad_maximum_fusion.19), channel_id=1, source_target_pairs={{0,9},{2,0},{4,2},{6,4},{14,6},{12,14},{10,12},{8,10},{1,8},{3,1},... | collective-permute-start | bytes 12296 | tf_op jit(solution)/shard_map/ppermute | solution.py:107
  126.3 4.3 %collective-permute-start.7 = (f32[1024]{0:T(1024)S(1)}, f32[1024]{0:T(1024)S(1)}, u32[]{:S(2)}, u32[]{:S(2)}) collective-permute-start(f32[1024]{0:T(1024)S(1)} %pad_maximum_fusion.18), channel_id=1, source_target_pairs={{0,12},{2,10},{4,8},{6,1},{14,3},{12,5},{10,7},{8,15},{1,13},{3,11... | collective-permute-start | bytes 12296 | tf_op jit(solution)/shard_map/ppermute | solution.py:107
  128.0 3.0 %collective-permute-start.6 = (f32[1024]{0:T(1024)S(1)}, f32[1024]{0:T(1024)S(1)}, u32[]{:S(2)}, u32[]{:S(2)}) collective-permute-start(f32[1024]{0:T(1024)S(1)} %pad_maximum_fusion.17), channel_id=1, source_target_pairs={{0,2},{2,4},{4,6},{6,14},{14,12},{12,10},{10,8},{8,1},{1,3},{3,5},... | collective-permute-start | bytes 12296 | tf_op jit(solution)/shard_map/ppermute | solution.py:107
  128.0 3.0 %collective-permute-start.4 = (f32[1024]{0:T(1024)S(1)}, f32[1024]{0:T(1024)S(1)}, u32[]{:S(2)}, u32[]{:S(2)}) collective-permute-start(f32[1024]{0:T(1024)S(1)} %pad_maximum_fusion.16), channel_id=1, source_target_pairs={{0,1},{2,3},{4,5},{6,7},{14,15},{12,13},{10,11},{8,9},{1,0},{3,2},... | collective-permute-start | bytes 12296 | tf_op jit(solution)/shard_map/ppermute | solution.py:107
  132.9 19.4 %all-to-all-start = ((f32[128,1,1]{2,1,0:T(1,128)}), f32[128,1,1]{2,1,0:T(1,128)S(1)}, u32[]{:S(2)}, u32[]{:S(2)}) async-start(f32[128,1,1]{2,1,0:T(1,128)} %broadcast_in_dim.9), calls=%async_computation | async-start | bytes 131072 | tf_op jit(solution)/shard_map/all_to_all | solution.py:68

commit v6 on v5

--- a/solution.py
+++ b/solution.py
@@ -87,10 +87,7 @@
     per_device = row_count // BLK
     order = lax.dynamic_slice_in_dim(block_order[0], position * per_device, per_device)
     blocks = embeddings.reshape(per_device, BLK, width)
-    pick = (order[:, None] == jnp.arange(per_device, dtype=jnp.int32)[None, :]).astype(embeddings.dtype)
-    ordered = jnp.einsum(
-        "sl,lrd->srd", pick, blocks, preferred_element_type=jnp.float32
-    ).astype(embeddings.dtype).reshape(row_count, width)
+    ordered = blocks.at[order].get(mode="promise_in_bounds").reshape(row_count, width)
     spans = [(start * BLK, end * BLK) for start, end in class_spans(per_device)]
 
     ring = member_ring(member_count)

time: 156 us -> 120 us (0.77)
  matrix products: 35.9 us -> 13.1 us
  local copies, waits for them, and re-layouts: 19.6 us -> 3.87 us
  waiting for transfers between devices: 65.8 us -> 74.6 us
  other arithmetic: 10.3 us -> 5.02 us
    dot_general x24, matrix products: 34.8 us -> 13.1 us  [kernel_sums(): lax.dot_general(left, right, (((1,), (1,)), ((), ())), preferred_element_...]
    slice x9 -> x11, local copies, waits for them, and re-layouts: 9.83 us -> 0.47 us  [blocks(): held[b][start:end]]
    ppermute x5, waiting for transfers between devices: 53.9 us -> 62.7 us  [fetch(): lax.ppermute(value, 'mem', [(ring[(r + offset) % member_count], ring[r])...]
    reduce_sum x5 -> x6, other arithmetic: 8.07 us -> 1.95 us  [squared(): return jnp.sum(jnp.square(values.astype(jnp.float32)), axis=1)]
    slice x5 -> x2, local copies, waits for them, and re-layouts: 3.61 us -> 0.13 us  [blocks(): held[a][start:end]]
  transfers between devices with their start and end apart: 10 -> 10, of which waited for: 5 -> 5; matrix products, arithmetic and copies ran while one was open for 11% -> 3% of each run, Pallas kernels for 0% -> 0%
where the time goes in v6:
time: 120 us
  waiting for transfers between devices  74.6 us (62%)
  starting transfers between devices  21.9 us (18%)
  matrix products  13.1 us (11%)
  other arithmetic  5.02 us (4%)
  local copies, waits for them, and re-layouts  3.87 us (3%)
    ppermute x5, waiting for transfers between devices, fetch(): lax.ppermute(value, 'mem', [(ring[(r + offset) % member_count], ring[r])...  62.7 us
    dot_general x24, matrix products, kernel_sums(): lax.dot_general(left, right, (((1,), (1,)), ((), ())), preferred_element_...  13.1 us
    all_to_all x1, starting transfers between devices, grand_total(): lax.all_to_all(jnp.broadcast_to(value, (size,)), axes, 0, 0, tiled=True)  9.82 us
    all_to_all x1, waiting for transfers between devices, grand_total(): lax.all_to_all(jnp.broadcast_to(value, (size,)), axes, 0, 0, tiled=True)  8.97 us
    ppermute x5, starting transfers between devices, fetch(): lax.ppermute(value, 'mem', [(ring[(r + offset) % member_count], ring[r])...  8.22 us
    ppermute x4, starting transfers between devices, give_back(): lax.ppermute(value, 'mem', [(ring[r], ring[(r + offset) % member_count])...  3.86 us
    ppermute x4, waiting for transfers between devices, give_back(): lax.ppermute(value, 'mem', [(ring[r], ring[(r + offset) % member_count])...  2.9 us
  transfers between devices with their start and end apart: 10, of which 5 were waited for; matrix products, arithmetic and copies ran while one was open for 3% of the time, Pallas kernels for 0%

profile of v6, /device:TPU:0, one launch (start us, length us, event | category | flops | bytes accessed | tf_op | source)
XLA Modules:
  0.0 119.6 jit_solution(8599300013715176707)
XLA Ops:
  0.0 0.8 fusion.62
  0.9 0.6 copy-done
  1.4 0.6 gather_fusion
  2.2 4.3 %collective-permute-start.2 = (bf16[1024,768]{1,0:T(8,128)(2,1)S(1)}, bf16[1024,768]{1,0:T(8,128)(2,1)S(1)}, u32[]{:S(2)}, u32[]{:S(2)}) collective-permute-start(bf16[1024,768]{1,0:T(8,128)(2,1)S(1)} %bitcast.55), channel_id=1, source_target_pairs={{12,0},{10,2},{8,4},{1,6},{3,14},{5,12},{7,10},{15,8},{13,1},{11,3... | collective-permute-start | bytes 4718600 | tf_op jit(solution)/shard_map/ppermute | solution.py:97
  6.4 1.0 collective-permute-start.1
  7.6 1.1 collective-permute-start.5
  8.6 1.8 %collective-permute-start.3 = (bf16[512,768]{1,0:T(8,128)(2,1)S(1)}, bf16[512,768]{1,0:T(8,128)(2,1)S(1)}, u32[]{:S(2)}, u32[]{:S(2)}) collective-permute-start(bf16[512,768]{1,0:T(8,128)(2,1)S(1)} %bitcast.57), channel_id=1, source_target_pairs={{9,0},{0,2},{2,4},{4,6},{6,14},{14,12},{12,10},{10,8},{8,1},{1,3},... | collective-permute-start | bytes 2359304 | tf_op jit(solution)/shard_map/ppermute | solution.py:97
  11.4 0.7 fusion.6
  12.6 46.1 %collective-permute-done.5 = bf16[512,768]{1,0:T(8,128)(2,1)S(1)} collective-permute-done((bf16[512,768]{1,0:T(8,128)(2,1)S(1)}, bf16[512,768]{1,0:T(8,128)(2,1)S(1)}, u32[]{:S(2)}, u32[]{:S(2)}) %collective-permute-start.5) | collective-permute-done | bytes 786464 | tf_op jit(solution)/shard_map/ppermute | solution.py:97
  59.0 16.6 %collective-permute-done.3 = bf16[512,768]{1,0:T(8,128)(2,1)S(1)} collective-permute-done((bf16[512,768]{1,0:T(8,128)(2,1)S(1)}, bf16[512,768]{1,0:T(8,128)(2,1)S(1)}, u32[]{:S(2)}, u32[]{:S(2)}) %collective-permute-start.3) | collective-permute-done | bytes 786464 | tf_op jit(solution)/shard_map/ppermute | solution.py:97
  77.3 1.3 %fusion.95 = (f32[1024]{0:T(1024)S(1)}, f32[512]{0:T(512)S(1)}) fusion(bf16[512,768]{1,0:T(8,128)(2,1)S(1)} %bitcast.59, bf16[512,768]{1,0:T(8,128)(2,1)S(1)} %slice.364, bf16[512,768]{1,0:T(8,128)(2,1)S(1)} %slice.363, f32[1024]{0:T(1024)S(1)} %get-tuple-element.98, f32[512]{0:T(512)S(1)} %slice_bitcast_fusion.12), kind=kOutput, calls=%fused_computation.194 | convolution fusion | flops 811596288 | bytes 2371584 | tf_op jit(solution)/shard_map/dot_general | solution.py:73
  78.6 0.7 exponential_reduce_fusion
  79.4 0.5 fusion.97
  80.0 0.4 fusion.99
  80.7 0.4 fusion.98
  82.9 0.8 fusion.28
  83.8 1.3 %fusion.93 = (f32[512]{0:T(512)S(1)}, f32[1024]{0:T(1024)S(1)}) fusion(bf16[512,768]{1,0:T(8,128)(2,1)S(1)} %collective-permute-done.3, bf16[512,768]{1,0:T(8,128)(2,1)S(1)} %slice.364, bf16[512,768]{1,0:T(8,128)(2,1)S(1)} %slice.363, f32[1024]{0:T(1024)S(1)} %get-tuple-element.98, f32[512]{0:T(512)S(1)} %multiply_reduce_fusion.5), kind=kOutput, calls=%fused_computation.192 | convolution fusion | flops 811596288 | bytes 2371584 | tf_op jit(solution)/shard_map/dot_general | solution.py:73
  85.1 1.3 %fusion.94 = (f32[1024]{0:T(1024)S(1)}, f32[512]{0:T(512)S(1)}) fusion(bf16[512,768]{1,0:T(8,128)(2,1)S(1)} %slice-done, bf16[512,768]{1,0:T(8,128)(2,1)S(1)} %slice.364, bf16[1024,768]{1,0:T(8,128)(2,1)S(1)} %collective-permute-done.1, f32[1024]{0:T(1024)S(1)} %get-tuple-element.97, f32[512]{0:T(512)S(1)} %slice.294), kind=kOutput, calls=%fused_computation.193 | convolution fusion | flops 811596288 | bytes 2371584 | tf_op jit(solution)/shard_map/dot_general | solution.py:73
  86.5 0.4 fusion.42
  87.5 0.5 fusion.33
  88.5 0.4 fusion.51
  88.9 0.5 fusion.96
  89.5 2.1 %collective-permute-start.8 = (f32[1024]{0:T(1024)S(1)}, f32[1024]{0:T(1024)S(1)}, u32[]{:S(2)}, u32[]{:S(2)}) collective-permute-start(f32[1024]{0:T(1024)S(1)} %pad_maximum_fusion.19), channel_id=1, source_target_pairs={{0,9},{2,0},{4,2},{6,4},{14,6},{12,14},{10,12},{8,10},{1,8},{3,1},... | collective-permute-start | bytes 12296 | tf_op jit(solution)/shard_map/ppermute | solution.py:104
  91.6 1.6 %collective-permute-start.7 = (f32[1024]{0:T(1024)S(1)}, f32[1024]{0:T(1024)S(1)}, u32[]{:S(2)}, u32[]{:S(2)}) collective-permute-start(f32[1024]{0:T(1024)S(1)} %pad_maximum_fusion.18), channel_id=1, source_target_pairs={{0,12},{2,10},{4,8},{6,1},{14,3},{12,5},{10,7},{8,15},{1,13},{3,11... | collective-permute-start | bytes 12296 | tf_op jit(solution)/shard_map/ppermute | solution.py:104
  93.4 2.5 %collective-permute-done.7 = f32[1024]{0:T(1024)S(1)} collective-permute-done((f32[1024]{0:T(1024)S(1)}, f32[1024]{0:T(1024)S(1)}, u32[]{:S(2)}, u32[]{:S(2)}) %collective-permute-start.7) | collective-permute-done | bytes 4128 | tf_op jit(solution)/shard_map/ppermute | solution.py:104
  96.3 0.6 fusion.100
  96.9 1.3 %broadcast_in_dim.12 = f32[128,1,1]{2,1,0:T(1,128)} broadcast(f32[]{:T(128)} %get-tuple-element.71), dimensions={} | broadcast | bytes 516 | tf_op jit(solution)/shard_map/broadcast_in_dim | solution.py:68
  98.2 9.8 %all-to-all-start = ((f32[128,1,1]{2,1,0:T(1,128)}), f32[128,1,1]{2,1,0:T(1,128)S(1)}, u32[]{:S(2)}, u32[]{:S(2)}) async-start(f32[128,1,1]{2,1,0:T(1,128)} %broadcast_in_dim.12), calls=%async_computation | async-start | bytes 131072 | tf_op jit(solution)/shard_map/all_to_all | solution.py:68
  108.1 0.6 gather_fusion.1
  108.6 9.0 %all-to-all-done = f32[128,1,1]{2,1,0:T(1,128)S(1)} async-done(((f32[128,1,1]{2,1,0:T(1,128)}), f32[128,1,1]{2,1,0:T(1,128)S(1)}, u32[]{:S(2)}, u32[]{:S(2)}) %all-to-all-start) | async-done | bytes 544 | tf_op jit(solution)/shard_map/all_to_all | solution.py:68
  117.6 0.7 reduce_sum.492
  119.0 0.6 multiply_bitcast_fusion
  (85 shorter events, 7.2 us)
Async XLA Ops:
  0.0 1.4 %copy-start = (bf16[1024,768]{1,0:T(8,128)(2,1)S(1)}, bf16[1024,768]{1,0:T(8,128)(2,1)}, u32[]{:S(2)}) copy-start(bf16[1024,768]{1,0:T(8,128)(2,1)} %param.2) | copy-start | bytes 4718596
  2.1 73.8 %collective-permute-start = (bf16[1024,768]{1,0:T(8,128)(2,1)S(1)}, bf16[1024,768]{1,0:T(8,128)(2,1)S(1)}, u32[]{:S(2)}, u32[]{:S(2)}) collective-permute-start(bf16[1024,768]{1,0:T(8,128)(2,1)S(1)} %bitcast.54), channel_id=1, source_target_pairs={{1,0},{3,2},{5,4},{7,6},{15,14},{13,12},{11,10},{9,8},{0,1},{2,3},... | collective-permute-start | bytes 4718600 | tf_op jit(solution)/shard_map/ppermute | solution.py:97
  2.2 74.1 %collective-permute-start.2 = (bf16[1024,768]{1,0:T(8,128)(2,1)S(1)}, bf16[1024,768]{1,0:T(8,128)(2,1)S(1)}, u32[]{:S(2)}, u32[]{:S(2)}) collective-permute-start(bf16[1024,768]{1,0:T(8,128)(2,1)S(1)} %bitcast.55), channel_id=1, source_target_pairs={{12,0},{10,2},{8,4},{1,6},{3,14},{5,12},{7,10},{15,8},{13,1},{11,3... | collective-permute-start | bytes 4718600 | tf_op jit(solution)/shard_map/ppermute | solution.py:97
  6.4 70.3 %collective-permute-start.1 = (bf16[1024,768]{1,0:T(8,128)(2,1)S(1)}, bf16[1024,768]{1,0:T(8,128)(2,1)S(1)}, u32[]{:S(2)}, u32[]{:S(2)}) collective-permute-start(bf16[1024,768]{1,0:T(8,128)(2,1)S(1)} %bitcast.56), channel_id=1, source_target_pairs={{2,0},{4,2},{6,4},{14,6},{12,14},{10,12},{8,10},{1,8},{3,1},{5,3},... | collective-permute-start | bytes 4718600 | tf_op jit(solution)/shard_map/ppermute | solution.py:97
  7.6 3.8 %copy-start.4 = (s32[1,128]{1,0:T(1,128)S(1)}, s32[1,128]{1,0:T(1,128)}, u32[]{:S(2)}) copy-start(s32[1,128]{1,0:T(1,128)} %param.3) | copy-start | bytes 1540
  7.6 51.2 %collective-permute-start.5 = (bf16[512,768]{1,0:T(8,128)(2,1)S(1)}, bf16[512,768]{1,0:T(8,128)(2,1)S(1)}, u32[]{:S(2)}, u32[]{:S(2)}) collective-permute-start(bf16[512,768]{1,0:T(8,128)(2,1)S(1)} %bitcast.61), channel_id=1, source_target_pairs={{9,0},{0,2},{2,4},{4,6},{6,14},{14,12},{12,10},{10,8},{8,1},{1,3},... | collective-permute-start | bytes 2359304 | tf_op jit(solution)/shard_map/ppermute | solution.py:97
  8.6 67.0 %collective-permute-start.3 = (bf16[512,768]{1,0:T(8,128)(2,1)S(1)}, bf16[512,768]{1,0:T(8,128)(2,1)S(1)}, u32[]{:S(2)}, u32[]{:S(2)}) collective-permute-start(bf16[512,768]{1,0:T(8,128)(2,1)S(1)} %bitcast.57), channel_id=1, source_target_pairs={{9,0},{0,2},{2,4},{4,6},{6,14},{14,12},{12,10},{10,8},{8,1},{1,3},... | collective-permute-start | bytes 2359304 | tf_op jit(solution)/shard_map/ppermute | solution.py:97
  59.0 17.7 %copy-start.3 = (f32[512]{0:T(512)}, f32[512]{0:T(512)S(1)}, u32[]{:S(2)}) copy-start(f32[512]{0:T(512)S(1)} %multiply_reduce_fusion.4) | copy-start | bytes 6148
  75.8 7.1 %copy-start.1 = (bf16[1024,768]{1,0:T(8,128)(2,1)}, bf16[1024,768]{1,0:T(8,128)(2,1)S(1)}, u32[]{:S(2)}) copy-start(bf16[1024,768]{1,0:T(8,128)(2,1)S(1)} %collective-permute-done) | copy-start | bytes 4718596
  83.7 1.3 %slice-start = ((bf16[1024,768]{1,0:T(8,128)(2,1)}), bf16[512,768]{1,0:T(8,128)(2,1)S(1)}, s32[]{:S(2)}) async-start(bf16[1024,768]{1,0:T(8,128)(2,1)} %copy-done.1), calls=%async_computation.1 | async-start | bytes 1572864 | tf_op jit(solution)/shard_map/slice | solution.py:142
  85.1 1.4 %copy-start.2 = (bf16[1024,768]{1,0:T(8,128)(2,1)S(1)}, bf16[1024,768]{1,0:T(8,128)(2,1)}, u32[]{:S(2)}) copy-start(bf16[1024,768]{1,0:T(8,128)(2,1)} %copy-done.1) | copy-start | bytes 4718596
  86.5 1.0 slice-start.1
  88.0 0.9 slice-start.2
  89.5 4.0 %collective-permute-start.8 = (f32[1024]{0:T(1024)S(1)}, f32[1024]{0:T(1024)S(1)}, u32[]{:S(2)}, u32[]{:S(2)}) collective-permute-start(f32[1024]{0:T(1024)S(1)} %pad_maximum_fusion.19), channel_id=1, source_target_pairs={{0,9},{2,0},{4,2},{6,4},{14,6},{12,14},{10,12},{8,10},{1,8},{3,1},... | collective-permute-start | bytes 12296 | tf_op jit(solution)/shard_map/ppermute | solution.py:104
  91.6 4.3 %collective-permute-start.7 = (f32[1024]{0:T(1024)S(1)}, f32[1024]{0:T(1024)S(1)}, u32[]{:S(2)}, u32[]{:S(2)}) collective-permute-start(f32[1024]{0:T(1024)S(1)} %pad_maximum_fusion.18), channel_id=1, source_target_pairs={{0,12},{2,10},{4,8},{6,1},{14,3},{12,5},{10,7},{8,15},{1,13},{3,11... | collective-permute-start | bytes 12296 | tf_op jit(solution)/shard_map/ppermute | solution.py:104
  93.3 3.0 %collective-permute-start.6 = (f32[1024]{0:T(1024)S(1)}, f32[1024]{0:T(1024)S(1)}, u32[]{:S(2)}, u32[]{:S(2)}) collective-permute-start(f32[1024]{0:T(1024)S(1)} %pad_maximum_fusion.17), channel_id=1, source_target_pairs={{0,2},{2,4},{4,6},{6,14},{14,12},{12,10},{10,8},{8,1},{1,3},{3,5},... | collective-permute-start | bytes 12296 | tf_op jit(solution)/shard_map/ppermute | solution.py:104
  93.3 3.0 %collective-permute-start.4 = (f32[1024]{0:T(1024)S(1)}, f32[1024]{0:T(1024)S(1)}, u32[]{:S(2)}, u32[]{:S(2)}) collective-permute-start(f32[1024]{0:T(1024)S(1)} %pad_maximum_fusion.16), channel_id=1, source_target_pairs={{0,1},{2,3},{4,5},{6,7},{14,15},{12,13},{10,11},{8,9},{1,0},{3,2},... | collective-permute-start | bytes 12296 | tf_op jit(solution)/shard_map/ppermute | solution.py:104
  98.2 19.4 %all-to-all-start = ((f32[128,1,1]{2,1,0:T(1,128)}), f32[128,1,1]{2,1,0:T(1,128)S(1)}, u32[]{:S(2)}, u32[]{:S(2)}) async-start(f32[128,1,1]{2,1,0:T(1,128)} %broadcast_in_dim.12), calls=%async_computation | async-start | bytes 131072 | tf_op jit(solution)/shard_map/all_to_all | solution.py:68

commit v7 on v6

--- a/solution.py
+++ b/solution.py
@@ -108,7 +108,7 @@
         )
 
     late = offsets[-1]
-    cut = spans[0][1]
+    cut = spans[1][1]
     held = {0: ordered}
     for offset in offsets[1:]:
         if offset == late:
@@ -157,9 +157,9 @@
 
     late_pairs = [p for p in pairs if late in p[:2]]
     blocks([(0, 0, False)] + [p for p in pairs if late not in p[:2]])
-    blocks(late_pairs, {0})
+    blocks(late_pairs, {0, 1})
     partial = lax.optimization_barrier(partial)
-    blocks(late_pairs, set(range(1, len(spans))))
+    blocks(late_pairs, set(range(2, len(spans))))
 
     def joined(offset):
         parts = [

time: 120 us -> 120 us (level)
  no operation moved by 1% of the time
where the time goes in v7:
time: 120 us
  waiting for transfers between devices  73.6 us (61%)
  starting transfers between devices  22.4 us (19%)
  matrix products  13.1 us (11%)
  other arithmetic  5.02 us (4%)
  local copies, waits for them, and re-layouts  4.16 us (3%)
    ppermute x5, waiting for transfers between devices, fetch(): lax.ppermute(value, 'mem', [(ring[(r + offset) % member_count], ring[r])...  61.8 us
    dot_general x24, matrix products, kernel_sums(): lax.dot_general(left, right, (((1,), (1,)), ((), ())), preferred_element_...  13.1 us
    all_to_all x1, starting transfers between devices, grand_total(): lax.all_to_all(jnp.broadcast_to(value, (size,)), axes, 0, 0, tiled=True)  9.46 us
    all_to_all x1, waiting for transfers between devices, grand_total(): lax.all_to_all(jnp.broadcast_to(value, (size,)), axes, 0, 0, tiled=True)  8.97 us
    ppermute x5, starting transfers between devices, fetch(): lax.ppermute(value, 'mem', [(ring[(r + offset) % member_count], ring[r])...  8 us
    ppermute x4, starting transfers between devices, give_back(): lax.ppermute(value, 'mem', [(ring[r], ring[(r + offset) % member_count])...  4.97 us
    ppermute x4, waiting for transfers between devices, give_back(): lax.ppermute(value, 'mem', [(ring[r], ring[(r + offset) % member_count])...  2.9 us
  transfers between devices with their start and end apart: 10, of which 5 were waited for; matrix products, arithmetic and copies ran while one was open for 3% of the time, Pallas kernels for 0%

profile of v7, /device:TPU:0, one launch (start us, length us, event | category | flops | bytes accessed | tf_op | source)
XLA Modules:
  0.0 119.5 jit_solution(4900629305086917143)
XLA Ops:
  0.0 0.8 fusion.65
  0.9 0.6 copy-done
  1.4 0.6 gather_fusion
  2.1 3.7 %collective-permute-start.2 = (bf16[1024,768]{1,0:T(8,128)(2,1)S(1)}, bf16[1024,768]{1,0:T(8,128)(2,1)S(1)}, u32[]{:S(2)}, u32[]{:S(2)}) collective-permute-start(bf16[1024,768]{1,0:T(8,128)(2,1)S(1)} %bitcast.54), channel_id=1, source_target_pairs={{12,0},{10,2},{8,4},{1,6},{3,14},{5,12},{7,10},{15,8},{13,1},{11,3... | collective-permute-start | bytes 4718600 | tf_op jit(solution)/shard_map/ppermute | solution.py:97
  5.7 1.0 collective-permute-start.1
  6.8 1.0 collective-permute-start
  7.8 0.5 collective-permute-start.5
  8.4 1.8 %collective-permute-start.3 = (bf16[768,768]{1,0:T(8,128)(2,1)S(1)}, bf16[768,768]{1,0:T(8,128)(2,1)S(1)}, u32[]{:S(2)}, u32[]{:S(2)}) collective-permute-start(bf16[768,768]{1,0:T(8,128)(2,1)S(1)} %bitcast.57), channel_id=1, source_target_pairs={{9,0},{0,2},{2,4},{4,6},{6,14},{14,12},{12,10},{10,8},{8,1},{1,3},... | collective-permute-start | bytes 3538952 | tf_op jit(solution)/shard_map/ppermute | solution.py:97
  10.9 0.7 fusion.6
  12.5 36.7 %collective-permute-done.5 = bf16[256,768]{1,0:T(8,128)(2,1)S(1)} collective-permute-done((bf16[256,768]{1,0:T(8,128)(2,1)S(1)}, bf16[256,768]{1,0:T(8,128)(2,1)S(1)}, u32[]{:S(2)}, u32[]{:S(2)}) %collective-permute-start.5) | collective-permute-done | bytes 393248 | tf_op jit(solution)/shard_map/ppermute | solution.py:97
  49.4 25.0 %collective-permute-done.3 = bf16[768,768]{1,0:T(8,128)(2,1)S(1)} collective-permute-done((bf16[768,768]{1,0:T(8,128)(2,1)S(1)}, bf16[768,768]{1,0:T(8,128)(2,1)S(1)}, u32[]{:S(2)}, u32[]{:S(2)}) %collective-permute-start.3) | collective-permute-done | bytes 1179680 | tf_op jit(solution)/shard_map/ppermute | solution.py:97
  76.2 1.3 %fusion.98 = (f32[1024]{0:T(1024)S(1)}, f32[512]{0:T(512)S(1)}) fusion(bf16[512,768]{1,0:T(8,128)(2,1)S(1)} %bitcast.59, bf16[512,768]{1,0:T(8,128)(2,1)S(1)} %slice.379, bf16[512,768]{1,0:T(8,128)(2,1)S(1)} %slice.378, f32[1024]{0:T(1024)S(1)} %get-tuple-element.98, f32[512]{0:T(512)S(1)} %slice_bitcast_fusion.12), kind=kOutput, calls=%fused_computation.193 | convolution fusion | flops 811596288 | bytes 2371584 | tf_op jit(solution)/shard_map/dot_general | solution.py:73
  77.5 0.7 exponential_reduce_fusion
  78.3 0.5 fusion.100
  80.0 0.4 fusion.103
  82.2 0.8 fusion.34
  83.0 1.3 %fusion.96 = (f32[512]{0:T(512)S(1)}, f32[1024]{0:T(1024)S(1)}) fusion(bf16[512,768]{1,0:T(8,128)(2,1)S(1)} %slice.379, bf16[512,768]{1,0:T(8,128)(2,1)S(1)} %slice.378, bf16[768,768]{1,0:T(8,128)(2,1)S(1)} %collective-permute-done.3, f32[1024]{0:T(1024)S(1)} %get-tuple-element.98, f32[512]{0:T(512)S(1)} %slice-done.2), kind=kOutput, calls=%fused_computation.191 | convolution fusion | flops 811596288 | bytes 2371584 | tf_op jit(solution)/shard_map/dot_general | solution.py:73
  84.4 1.3 %fusion.97 = (f32[1024]{0:T(1024)S(1)}, f32[512]{0:T(512)S(1)}) fusion(bf16[512,768]{1,0:T(8,128)(2,1)S(1)} %slice-done, bf16[512,768]{1,0:T(8,128)(2,1)S(1)} %slice.379, bf16[1024,768]{1,0:T(8,128)(2,1)S(1)} %collective-permute-done.1, f32[1024]{0:T(1024)S(1)} %get-tuple-element.97, f32[512]{0:T(512)S(1)} %slice.305), kind=kOutput, calls=%fused_computation.192 | convolution fusion | flops 811596288 | bytes 2371584 | tf_op jit(solution)/shard_map/dot_general | solution.py:73
  85.8 0.4 fusion.49
  86.2 0.5 fusion.99
  86.8 0.4 slice-done.1
  87.2 0.5 fusion.40
  88.6 3.3 %collective-permute-start.8 = (f32[1024]{0:T(1024)S(1)}, f32[1024]{0:T(1024)S(1)}, u32[]{:S(2)}, u32[]{:S(2)}) collective-permute-start(f32[1024]{0:T(1024)S(1)} %pad_maximum_fusion.19), channel_id=1, source_target_pairs={{0,9},{2,0},{4,2},{6,4},{14,6},{12,14},{10,12},{8,10},{1,8},{3,1},... | collective-permute-start | bytes 12296 | tf_op jit(solution)/shard_map/ppermute | solution.py:104
  91.9 1.6 %collective-permute-start.7 = (f32[1024]{0:T(1024)S(1)}, f32[1024]{0:T(1024)S(1)}, u32[]{:S(2)}, u32[]{:S(2)}) collective-permute-start(f32[1024]{0:T(1024)S(1)} %pad_maximum_fusion.18), channel_id=1, source_target_pairs={{0,12},{2,10},{4,8},{6,1},{14,3},{12,5},{10,7},{8,15},{1,13},{3,11... | collective-permute-start | bytes 12296 | tf_op jit(solution)/shard_map/ppermute | solution.py:104
  93.7 2.6 %collective-permute-done.7 = f32[1024]{0:T(1024)S(1)} collective-permute-done((f32[1024]{0:T(1024)S(1)}, f32[1024]{0:T(1024)S(1)}, u32[]{:S(2)}, u32[]{:S(2)}) %collective-permute-start.7) | collective-permute-done | bytes 4128 | tf_op jit(solution)/shard_map/ppermute | solution.py:104
  96.6 0.6 fusion.105
  97.2 1.3 %broadcast_in_dim.12 = f32[128,1,1]{2,1,0:T(1,128)} broadcast(f32[]{:T(128)} %get-tuple-element.73), dimensions={} | broadcast | bytes 516 | tf_op jit(solution)/shard_map/broadcast_in_dim | solution.py:68
  98.5 9.5 %all-to-all-start = ((f32[128,1,1]{2,1,0:T(1,128)}), f32[128,1,1]{2,1,0:T(1,128)S(1)}, u32[]{:S(2)}, u32[]{:S(2)}) async-start(f32[128,1,1]{2,1,0:T(1,128)} %broadcast_in_dim.12), calls=%async_computation | async-start | bytes 131072 | tf_op jit(solution)/shard_map/all_to_all | solution.py:68
  108.0 0.6 gather_fusion.1
  108.5 9.0 %all-to-all-done = f32[128,1,1]{2,1,0:T(1,128)S(1)} async-done(((f32[128,1,1]{2,1,0:T(1,128)}), f32[128,1,1]{2,1,0:T(1,128)S(1)}, u32[]{:S(2)}, u32[]{:S(2)}) %all-to-all-start) | async-done | bytes 544 | tf_op jit(solution)/shard_map/all_to_all | solution.py:68
  117.5 0.7 reduce_sum.492
  118.9 0.6 multiply_bitcast_fusion
  (87 shorter events, 7.7 us)
Async XLA Ops:
  0.0 1.4 %copy-start = (bf16[1024,768]{1,0:T(8,128)(2,1)S(1)}, bf16[1024,768]{1,0:T(8,128)(2,1)}, u32[]{:S(2)}) copy-start(bf16[1024,768]{1,0:T(8,128)(2,1)} %param.2) | copy-start | bytes 4718596
  2.1 73.1 %collective-permute-start.2 = (bf16[1024,768]{1,0:T(8,128)(2,1)S(1)}, bf16[1024,768]{1,0:T(8,128)(2,1)S(1)}, u32[]{:S(2)}, u32[]{:S(2)}) collective-permute-start(bf16[1024,768]{1,0:T(8,128)(2,1)S(1)} %bitcast.54), channel_id=1, source_target_pairs={{12,0},{10,2},{8,4},{1,6},{3,14},{5,12},{7,10},{15,8},{13,1},{11,3... | collective-permute-start | bytes 4718600 | tf_op jit(solution)/shard_map/ppermute | solution.py:97
  5.7 69.8 %collective-permute-start.1 = (bf16[1024,768]{1,0:T(8,128)(2,1)S(1)}, bf16[1024,768]{1,0:T(8,128)(2,1)S(1)}, u32[]{:S(2)}, u32[]{:S(2)}) collective-permute-start(bf16[1024,768]{1,0:T(8,128)(2,1)S(1)} %bitcast.55), channel_id=1, source_target_pairs={{2,0},{4,2},{6,4},{14,6},{12,14},{10,12},{8,10},{1,8},{3,1},{5,3},... | collective-permute-start | bytes 4718600 | tf_op jit(solution)/shard_map/ppermute | solution.py:97
  6.8 68.0 %collective-permute-start = (bf16[1024,768]{1,0:T(8,128)(2,1)S(1)}, bf16[1024,768]{1,0:T(8,128)(2,1)S(1)}, u32[]{:S(2)}, u32[]{:S(2)}) collective-permute-start(bf16[1024,768]{1,0:T(8,128)(2,1)S(1)} %bitcast.56), channel_id=1, source_target_pairs={{1,0},{3,2},{5,4},{7,6},{15,14},{13,12},{11,10},{9,8},{0,1},{2,3},... | collective-permute-start | bytes 4718600 | tf_op jit(solution)/shard_map/ppermute | solution.py:97
  7.8 41.4 %collective-permute-start.5 = (bf16[256,768]{1,0:T(8,128)(2,1)S(1)}, bf16[256,768]{1,0:T(8,128)(2,1)S(1)}, u32[]{:S(2)}, u32[]{:S(2)}) collective-permute-start(bf16[256,768]{1,0:T(8,128)(2,1)S(1)} %bitcast.64), channel_id=1, source_target_pairs={{9,0},{0,2},{2,4},{4,6},{6,14},{14,12},{12,10},{10,8},{8,1},{1,3},... | collective-permute-start | bytes 1179656 | tf_op jit(solution)/shard_map/ppermute | solution.py:97
  8.4 66.0 %collective-permute-start.3 = (bf16[768,768]{1,0:T(8,128)(2,1)S(1)}, bf16[768,768]{1,0:T(8,128)(2,1)S(1)}, u32[]{:S(2)}, u32[]{:S(2)}) collective-permute-start(bf16[768,768]{1,0:T(8,128)(2,1)S(1)} %bitcast.57), channel_id=1, source_target_pairs={{9,0},{0,2},{2,4},{4,6},{6,14},{14,12},{12,10},{10,8},{8,1},{1,3},... | collective-permute-start | bytes 3538952 | tf_op jit(solution)/shard_map/ppermute | solution.py:97
  10.9 1.0 copy-start.4
  74.7 0.8 copy-start.3
  74.7 7.5 %copy-start.1 = (bf16[1024,768]{1,0:T(8,128)(2,1)}, bf16[1024,768]{1,0:T(8,128)(2,1)S(1)}, u32[]{:S(2)}) copy-start(bf16[1024,768]{1,0:T(8,128)(2,1)S(1)} %collective-permute-done) | copy-start | bytes 4718596
  82.2 0.8 slice-start.2
  83.0 1.4 %slice-start = ((bf16[1024,768]{1,0:T(8,128)(2,1)}), bf16[512,768]{1,0:T(8,128)(2,1)S(1)}, s32[]{:S(2)}) async-start(bf16[1024,768]{1,0:T(8,128)(2,1)} %copy-done.1), calls=%async_computation.1 | async-start | bytes 1572864 | tf_op jit(solution)/shard_map/slice | solution.py:142
  84.4 1.4 %copy-start.2 = (bf16[1024,768]{1,0:T(8,128)(2,1)S(1)}, bf16[1024,768]{1,0:T(8,128)(2,1)}, u32[]{:S(2)}) copy-start(bf16[1024,768]{1,0:T(8,128)(2,1)} %copy-done.1) | copy-start | bytes 4718596
  86.2 1.0 slice-start.1
  88.6 5.0 %collective-permute-start.8 = (f32[1024]{0:T(1024)S(1)}, f32[1024]{0:T(1024)S(1)}, u32[]{:S(2)}, u32[]{:S(2)}) collective-permute-start(f32[1024]{0:T(1024)S(1)} %pad_maximum_fusion.19), channel_id=1, source_target_pairs={{0,9},{2,0},{4,2},{6,4},{14,6},{12,14},{10,12},{8,10},{1,8},{3,1},... | collective-permute-start | bytes 12296 | tf_op jit(solution)/shard_map/ppermute | solution.py:104
  91.9 4.3 %collective-permute-start.7 = (f32[1024]{0:T(1024)S(1)}, f32[1024]{0:T(1024)S(1)}, u32[]{:S(2)}, u32[]{:S(2)}) collective-permute-start(f32[1024]{0:T(1024)S(1)} %pad_maximum_fusion.18), channel_id=1, source_target_pairs={{0,12},{2,10},{4,8},{6,1},{14,3},{12,5},{10,7},{8,15},{1,13},{3,11... | collective-permute-start | bytes 12296 | tf_op jit(solution)/shard_map/ppermute | solution.py:104
  93.5 3.0 %collective-permute-start.6 = (f32[1024]{0:T(1024)S(1)}, f32[1024]{0:T(1024)S(1)}, u32[]{:S(2)}, u32[]{:S(2)}) collective-permute-start(f32[1024]{0:T(1024)S(1)} %pad_maximum_fusion.17), channel_id=1, source_target_pairs={{0,2},{2,4},{4,6},{6,14},{14,12},{12,10},{10,8},{8,1},{1,3},{3,5},... | collective-permute-start | bytes 12296 | tf_op jit(solution)/shard_map/ppermute | solution.py:104
  93.6 3.0 %collective-permute-start.4 = (f32[1024]{0:T(1024)S(1)}, f32[1024]{0:T(1024)S(1)}, u32[]{:S(2)}, u32[]{:S(2)}) collective-permute-start(f32[1024]{0:T(1024)S(1)} %pad_maximum_fusion.16), channel_id=1, source_target_pairs={{0,1},{2,3},{4,5},{6,7},{14,15},{12,13},{10,11},{8,9},{1,0},{3,2},... | collective-permute-start | bytes 12296 | tf_op jit(solution)/shard_map/ppermute | solution.py:104
  98.5 19.0 %all-to-all-start = ((f32[128,1,1]{2,1,0:T(1,128)}), f32[128,1,1]{2,1,0:T(1,128)S(1)}, u32[]{:S(2)}, u32[]{:S(2)}) async-start(f32[128,1,1]{2,1,0:T(1,128)} %broadcast_in_dim.12), calls=%async_computation | async-start | bytes 131072 | tf_op jit(solution)/shard_map/all_to_all | solution.py:68
